TPU v7x, 128 devices: a whole 4x4x4 slice. The times are simulated.
128 devices in a mesh: dp: 32 (over z, y, core), mp: 4 (over x).
Axes of the slice: x: 4, y: 4, z: 4, core: 2. Of those that a mesh axis runs over, the one named last changes fastest.
Arguments:
- tokens: bfloat16 [57344, 1024], P('dp'), may hold values from -60 to 60
- segment_ids: int32 [57344], P('dp'), may hold values from 0 to 127, as said below
- page_table: int32 [448], P('dp'), may hold values from 0 to 447, as said below
- w_query: bfloat16 [1024, 1024], P('dp', 'mp'), may hold values from -0.1875 to 0.1875
- w_key: bfloat16 [1024, 1024], P('dp', 'mp'), may hold values from -0.1875 to 0.1875
- w_value: bfloat16 [1024, 1024], P('dp', 'mp'), may hold values from -0.1875 to 0.1875
- w_out: bfloat16 [1024, 1024], P('mp', 'dp'), may hold values from -1.5 to 1.5
- w_up: bfloat16 [1024, 4096], P('dp', 'mp'), may hold values from -0.1875 to 0.1875
- w_down: bfloat16 [4096, 1024], P('mp', 'dp'), may hold values from -0.09375 to 0.09375
- gain_first: float32 [1024], replicated, may hold values from 0.1 to 1.9
- shift_first: float32 [1024], replicated, may hold values from -3 to 3
- gain_second: float32 [1024], replicated, may hold values from 0.1 to 1.9
- shift_second: float32 [1024], replicated, may hold values from -3 to 3
Outputs:
- mixed: bfloat16 [57344, 1024], P('dp')
- kv_cache: bfloat16 [57344, 2, 1024], P('dp', None, 'mp')
Inputs may be any that keep to these rules, and one draw needn't show every extreme that they name: page_table is a permutation of the page slots. Page p lies on device p // 14 in arrival order and goes to device page_table[p] // 14; from one device at most 1 pages go to one device, and some pair reaches 1. `segment_ids`: tokens with equal ids form one request; after dealing, a request's tokens are consecutive and lie on one device, which holds at most 4 requests.
All inputs are finite; a program needn't handle non-finite values.
Results may differ from a plain program's by a relative error of at most 0.014.
Values may be sent and summed in bfloat16 or wider, within the bound.
No kernel may reach another device: no remote copies, remote signals or barrier semaphores. Data moves between devices by JAX's collectives and lax.ppermute only.
A program may use at most 128 MiB of HBM per device.

v0:
```python
import jax
import jax.numpy as jnp
from jax import lax
from jax.experimental import pallas as pl
from jax.sharding import PartitionSpec as P

HEAD = 64


def layer_norm(hidden_sum, gain, shift):
    center = hidden_sum - jnp.mean(hidden_sum, axis=-1, keepdims=True)
    spread = jnp.mean(center * center, axis=-1, keepdims=True)
    return center * lax.rsqrt(spread + 1e-05) * gain + shift


def _attn_kernel(q_ref, k_ref, v_ref, qid_ref, kid_ref, o_ref):
    scores = lax.dot_general(
        q_ref[0], k_ref[0], (((1,), (1,)), ((), ())), preferred_element_type=jnp.float32
    ) * (HEAD ** -0.5)
    scores = jnp.where(qid_ref[...] == kid_ref[...], scores, -1e30)
    highest = jnp.max(scores, axis=1, keepdims=True)
    raised = jnp.exp(scores - highest)
    weights = (raised / jnp.sum(raised, axis=1, keepdims=True)).astype(jnp.bfloat16)
    o_ref[0] = jnp.dot(weights, v_ref[0], preferred_element_type=jnp.float32).astype(o_ref.dtype)


def attention(q, k, v, ids, block_q=256):
    heads, rows, dim = q.shape
    qid = ids.reshape(rows, 1)
    kid = ids.reshape(1, rows)
    return pl.pallas_call(
        _attn_kernel,
        out_shape=jax.ShapeDtypeStruct((heads, rows, dim), jnp.bfloat16),
        grid=(heads, rows // block_q),
        in_specs=[
            pl.BlockSpec((1, block_q, dim), lambda h, i: (h, i, 0)),
            pl.BlockSpec((1, rows, dim), lambda h, i: (h, 0, 0)),
            pl.BlockSpec((1, rows, dim), lambda h, i: (h, 0, 0)),
            pl.BlockSpec((block_q, 1), lambda h, i: (i, 0)),
            pl.BlockSpec((1, rows), lambda h, i: (0, 0)),
        ],
        out_specs=pl.BlockSpec((1, block_q, dim), lambda h, i: (h, i, 0)),
        cost_estimate=pl.CostEstimate(
            flops=4 * heads * rows * rows * dim,
            transcendentals=heads * rows * rows,
            bytes_accessed=4 * heads * rows * dim * 2,
        ),
    )(q, k, v, qid, kid)


def body(
    tokens,
    segment_ids,
    page_table,
    w_query,
    w_key,
    w_value,
    w_out,
    w_up,
    w_down,
    gain_first,
    shift_first,
    gain_second,
    shift_second,
):
    n_data = lax.axis_size("dp")
    n_model = lax.axis_size("mp")
    me_model = lax.axis_index("mp")
    pages_dev = page_table.shape[0]
    page = tokens.shape[0] // pages_dev
    width = tokens.shape[1]
    quarter = width // n_model
    sub = page // n_model
    slots_per = (pages_dev + n_data - 1) // n_data
    buffer_rows = n_data * slots_per

    head_cols = w_query.shape[1]
    in_part = w_out.shape[0]
    unit_part = w_up.shape[1]
    attn_local = jnp.concatenate([w_query, w_key, w_value], axis=1)
    attn_gathered = lax.all_gather(attn_local, "dp", axis=0, tiled=True)
    full_query = attn_gathered[:, :head_cols]
    full_key = attn_gathered[:, head_cols : 2 * head_cols]
    full_value = attn_gathered[:, 2 * head_cols : 3 * head_cols]
    small = jnp.concatenate([w_out.T, w_up, w_down.T], axis=1)

    target = page_table // pages_dev
    local_slot = page_table % pages_dev
    order = jnp.arange(pages_dev, dtype=jnp.int32)
    earlier = (target[:, None] == target[None, :]) & (order[:, None] < order[None, :])
    rank = jnp.sum(earlier.astype(jnp.int32), axis=0)
    position = target * slots_per + rank
    meta = jnp.zeros((pages_dev, 1, quarter), tokens.dtype)
    meta = meta.at[:, 0, :page].set(segment_ids.reshape(pages_dev, page).astype(tokens.dtype))
    meta = meta.at[:, 0, page].set(local_slot.astype(tokens.dtype))
    token_part = lax.dynamic_slice_in_dim(tokens, me_model * quarter, quarter, axis=1)
    with_meta = jnp.concatenate([token_part.reshape(pages_dev, page, quarter), meta], axis=1)
    send_pages = (
        jnp.zeros((buffer_rows, page + 1, quarter), tokens.dtype)
        .at[:, page, page]
        .set(-1)
        .at[position]
        .set(with_meta)
    )
    small, send_pages = lax.optimization_barrier((small, send_pages))
    got_all = lax.all_to_all(send_pages, "dp", split_axis=0, concat_axis=0, tiled=True)
    got_pages = got_all[:, :page]
    got_ids = got_all[:, page, :page].astype(jnp.int32)
    got_slots = got_all[:, page, page].astype(jnp.int32)
    matches = got_slots[None, :] == order[:, None]
    source_row = jnp.sum(
        jnp.where(matches, jnp.arange(buffer_rows, dtype=jnp.int32)[None, :], 0), axis=1
    )
    small_all = lax.all_gather(small, "mp", axis=1)
    rows_dp = small.shape[0]
    out_rows = small_all[:, :, :in_part].reshape(rows_dp, n_model * in_part)
    up_rows = small_all[:, :, in_part : in_part + unit_part].reshape(rows_dp, n_model * unit_part)
    down_rows = small_all[:, :, in_part + unit_part :].reshape(rows_dp, n_model * unit_part)
    ffn_local = jnp.concatenate([out_rows, up_rows, down_rows], axis=1)
    dealt_part = got_pages[source_row]
    dealt_part, attn_gathered = lax.optimization_barrier((dealt_part, attn_gathered))
    dealt = lax.all_gather(dealt_part, "mp", axis=2, tiled=True).reshape(pages_dev * page, width)
    dealt_ids = got_ids[source_row].reshape(pages_dev * page)
    ffn_local, dealt = lax.optimization_barrier((ffn_local, dealt))
    ffn_gathered = lax.all_gather(ffn_local, "dp", axis=0, tiled=True)
    units = n_model * unit_part
    in_all = n_model * in_part
    out_all_t = ffn_gathered[:, :in_all]
    full_up = ffn_gathered[:, in_all : in_all + units]
    down_t = ffn_gathered[:, in_all + units :]

    query = jnp.dot(dealt, full_query, preferred_element_type=jnp.float32).astype(jnp.bfloat16)
    keys = jnp.dot(dealt, full_key, preferred_element_type=jnp.float32).astype(jnp.bfloat16)
    values = jnp.dot(dealt, full_value, preferred_element_type=jnp.float32).astype(jnp.bfloat16)
    heads_here = query.shape[1] // HEAD
    rows = query.shape[0]

    def by_head(x):
        return x.reshape(rows, heads_here, HEAD).transpose(1, 0, 2)

    context = (
        attention(by_head(query), by_head(keys), by_head(values), dealt_ids)
        .transpose(1, 0, 2)
        .reshape(rows, heads_here * HEAD)
    )

    context_rows = lax.all_to_all(
        context.reshape(pages_dev, n_model, sub, head_cols),
        "mp",
        split_axis=1,
        concat_axis=1,
        tiled=True,
    )
    attended = jnp.zeros((pages_dev, sub, width), jnp.float32)
    for group in range(n_model):
        term = jnp.einsum(
            "pic,oc->pio",
            context_rows[:, group],
            out_all_t[:, group * head_cols : (group + 1) * head_cols],
            preferred_element_type=jnp.float32,
        ).astype(jnp.bfloat16)
        attended = attended + term.astype(jnp.float32)
    dealt_mine = lax.dynamic_index_in_dim(
        dealt.reshape(pages_dev, n_model, sub, width), me_model, axis=1, keepdims=False
    )
    first_mine = layer_norm(
        dealt_mine.astype(jnp.float32) + attended, gain_first, shift_first
    ).astype(jnp.bfloat16)
    hidden = jax.nn.gelu(
        jnp.einsum("pid,du->piu", first_mine, full_up, preferred_element_type=jnp.float32),
        approximate=False,
    ).astype(jnp.bfloat16)
    fed = jnp.zeros((pages_dev, sub, width), jnp.float32)
    for group in range(n_model):
        term = jnp.einsum(
            "piu,ou->pio",
            hidden[:, :, group * unit_part : (group + 1) * unit_part],
            down_t[:, group * unit_part : (group + 1) * unit_part],
            preferred_element_type=jnp.float32,
        ).astype(jnp.bfloat16)
        fed = fed + term.astype(jnp.float32)
    second_mine = layer_norm(first_mine.astype(jnp.float32) + fed, gain_second, shift_second).astype(
        jnp.bfloat16
    )

    valid = got_slots >= 0
    outgoing = jnp.where(
        valid[:, None, None],
        second_mine[jnp.clip(got_slots, 0, pages_dev - 1)],
        jnp.zeros((), second_mine.dtype),
    )
    returned = lax.all_to_all(outgoing, "dp", split_axis=0, concat_axis=0, tiled=True)
    mixed_mine = returned[position]
    mixed = lax.all_gather(mixed_mine, "mp", axis=1).reshape(pages_dev * page, width)
    kv_cache = jnp.stack([keys, values], axis=1)
    return (mixed, kv_cache)


def solution(mesh):
    return jax.shard_map(
        body,
        mesh=mesh,
        in_specs=(
            P("dp", None),
            P("dp"),
            P("dp"),
            P("dp", "mp"),
            P("dp", "mp"),
            P("dp", "mp"),
            P("mp", "dp"),
            P("dp", "mp"),
            P("mp", "dp"),
            P(),
            P(),
            P(),
            P(),
        ),
        out_specs=(P("dp", None), P("dp", None, "mp")),
        check_vma=False,
    )
```

profile of v0, /device:TPU:1, one launch (start us, length us, event | category | flops | bytes accessed | tf_op | source)
XLA Modules:
  0.0 329.3 jit_solution(5764991858791285280)
XLA Ops:
  7.2 1.4 pad_maximum_fusion.4
  10.0 0.7 convert_bitcast_fusion
  10.9 1.4 and_reduce_fusion
  12.2 1.4 broadcast_select_fusion.1
  13.6 0.8 scatter.24
  14.4 1.2 constant_dynamic-slice_fusion
  15.9 1.3 scatter_fusion
  17.3 40.9 %all_to_all.15 = bf16[32,129,256]{2,1,0:T(8,128)(2,1)S(1)} all-to-all(bf16[32,129,256]{2,1,0:T(8,128)(2,1)S(1)} %scatter_fusion), channel_id=1, replica_groups=mesh['dp'=32,'mp'=4] {'dp'}, dimensions={0} | all-to-all | bytes 4227072 | tf_op jit(solution)/shard_map/all_to_all | solution.py:106
  58.5 1.1 copy-done
  59.6 1.2 clamp_reduce_fusion
  60.9 1.5 gather_fusion
  62.5 2.9 all-gather.7.cloned.1.call-done
  65.4 11.5 %all-gather = bf16[32,9216]{1,0:T(8,128)(2,1)S(1)} all-gather(bf16[32,2304]{1,0:T(8,128)(2,1)S(1)} %pad_maximum_fusion.3), channel_id=2, replica_groups=mesh['dp'=32,'mp'=4] {'mp'}, dimensions={1}, use_global_device_ids=true | all-gather | bytes 737280 | tf_op jit(solution)/shard_map/all_gather | solution.py:114
  77.8 0.9 pad_maximum_fusion.2
  78.6 33.3 %all-gather.9.cloned.1.call-done = bf16[14,128,1024]{2,1,0:T(8,128)(2,1)} async-done(((bf16[14,128,256]{2,1,0:T(8,128)(2,1)}), bf16[14,128,1024]{2,1,0:T(8,128)(2,1)}) %all-gather.9.cloned.1.call-update) | async-done | bytes 3670032 | tf_op jit(solution)/shard_map/all_gather | solution.py:122
  111.9 0.9 slice_convert_fusion
  113.4 1.3 copy.51
  114.7 3.3 %convolution_convert_fusion.2 = bf16[1792,256]{0,1:T(8,128)(2,1)S(1)} fusion(bf16[1792,1024]{1,0:T(8,128)(2,1)} %bitcast.129, bf16[1024,768]{1,0:T(8,128)(2,1)} %all-gather.7.cloned.1.call-done), kind=kOutput, calls=%fused_computation.28 | convolution fusion | flops 939982848 | bytes 5111808 | tf_op jit(solution)/shard_map/dot_general | solution.py:132
  118.0 1.6 copy.39
  119.6 3.3 %convolution_convert_fusion.1 = bf16[1792,256]{0,1:T(8,128)(2,1)S(1)} fusion(bf16[1792,1024]{1,0:T(8,128)(2,1)} %bitcast.130, bf16[1024,768]{1,0:T(8,128)(2,1)} %all-gather.7.cloned.1.call-done), kind=kOutput, calls=%fused_computation.27 | convolution fusion | flops 939982848 | bytes 5111808 | tf_op jit(solution)/shard_map/dot_general | solution.py:133
  122.9 1.6 copy.40
  124.6 3.5 %convolution_convert_fusion = bf16[1792,256]{0,1:T(8,128)(2,1)S(1)} fusion(bf16[1792,1024]{1,0:T(8,128)(2,1)} %bitcast.131, bf16[1024,768]{1,0:T(8,128)(2,1)} %all-gather.7.cloned.1.call-done), kind=kOutput, calls=%fused_computation.26 | convolution fusion | flops 939982848 | bytes 5111808 | tf_op jit(solution)/shard_map/dot_general | solution.py:134
  128.2 1.7 copy.41
  129.9 38.5 %shard_map.140 = bf16[4,1792,64]{2,1,0:T(8,128)(2,1)} custom-call(bf16[4,1792,64]{2,1,0:T(8,128)(2,1)} %bitcast.117, bf16[4,1792,64]{2,1,0:T(8,128)(2,1)} %bitcast.118, bf16[4,1792,64]{2,1,0:T(8,128)(2,1)} %bitcast.119, s32[1792,1]{1,0:T(8,128)} %bitcast.124, s32[1,1792]{1,0:T(1,128)} %bitcast.136), custom_call_target="tpu_custom_call" | custom-call | flops 3288334336 | bytes 3670016 | tf_op jit(solution)/shard_map/pallas_call | solution.py:31
  168.4 8.8 %copy.43 = bf16[1792,4,64]{2,1,0:T(4,128)(2,1)S(1)} copy(bf16[1792,4,64]{2,0,1:T(8,128)(2,1)} %bitcast.116) | data formatting | bytes 1835008 | tf_op jit(solution)/shard_map/transpose | solution.py:143
  177.2 1.2 reshape_reshape.11
  178.4 1.0 copy.44
  179.4 3.7 %all-to-all-start.1 = ((bf16[14,4,32,256]{3,2,0,1:T(8,128)(2,1)}), bf16[14,4,32,256]{3,2,0,1:T(8,128)(2,1)S(1)}, u32[]{:S(2)}, u32[]{:S(2)}) async-start(bf16[14,4,32,256]{3,2,0,1:T(8,128)(2,1)} %copy.44), calls=%async_computation.1 | async-start | bytes 1835008 | tf_op jit(solution)/shard_map/all_to_all | solution.py:147
  183.2 1.5 compare_reduce_fusion
  184.7 9.4 %all-to-all-done.1 = bf16[14,4,32,256]{3,2,0,1:T(8,128)(2,1)S(1)} async-done(((bf16[14,4,32,256]{3,2,0,1:T(8,128)(2,1)}), bf16[14,4,32,256]{3,2,0,1:T(8,128)(2,1)S(1)}, u32[]{:S(2)}, u32[]{:S(2)}) %all-to-all-start.1) | async-done | bytes 917536 | tf_op jit(solution)/shard_map/all_to_all | solution.py:147
  194.4 1.5 convolution_convert_fusion.4
  195.9 1.5 convolution_convert_fusion.5
  197.4 1.5 convolution_convert_fusion.6
  198.9 2.2 fusion.33
  201.4 21.6 %fusion.3 = bf16[14,32,4096]{2,1,0:T(8,128)(2,1)S(1)} fusion(bf16[1024,9216]{1,0:T(8,128)(2,1)} %all-gather.11.cloned.1.call-done, f32[14,32,1024]{2,1,0:T(8,128)S(1)} %get-tuple-element.63, f32[1024]{0:T(1024)S(1)} %copy-done.11, f32[1024]{0:T(1024)S(1)} %copy-done.12, f32[14,32]{1,0:T(8,128)S(1)} %add_rsqrt_fusion.1, ...), kind=kOutput, calls=%fused_computation.10 | convolution fusion | flops 3879665664 | bytes 13905408 | tf_op jit(solution)/shard_map/pid,du->piu/dot_general | solution.py:170
  223.0 2.7 fusion.17
  225.8 2.7 fusion.16
  228.5 2.7 fusion.15
  231.3 3.3 %fusion.34 = (f32[14,32]{1,0:T(8,128)S(1)}, f32[14,32,1024]{2,1,0:T(8,128)S(1)}) fusion(bf16[1024,9216]{1,0:T(8,128)(2,1)} %all-gather.11.cloned.1.call-done, bf16[14,32,4096]{2,1,0:T(8,128)(2,1)S(1)} %fusion.3, bf16[14,32,1024]{2,1,0:T(8,128)(2,1)S(1)} %fusion.17, bf16[14,32,1024]{2,1,0:T(8,128)(2,1)S(1)} %fusion.16, ...), kind=kOutput, calls=%fused_computation.106 | convolution fusion | flops 946863680 | bytes 9463552 | tf_op jit(solution)/shard_map/piu,ou->pio/dot_general | solution.py:175
  235.4 0.7 gather_fusion.2
  236.1 1.5 broadcast_select_fusion
  237.6 10.5 %all-to-all-start.2 = ((bf16[32,32,1024]{2,1,0:T(8,128)(2,1)}), bf16[32,32,1024]{2,1,0:T(8,128)(2,1)S(1)}, u32[]{:S(2)}, u32[]{:S(2)}) async-start(bf16[32,32,1024]{2,1,0:T(8,128)(2,1)} %broadcast_select_fusion), calls=%async_computation.2 | async-start | bytes 4194304 | tf_op jit(solution)/shard_map/all_to_all | solution.py:192
  248.2 28.5 %all-to-all-done.2 = bf16[32,32,1024]{2,1,0:T(8,128)(2,1)S(1)} async-done(((bf16[32,32,1024]{2,1,0:T(8,128)(2,1)}), bf16[32,32,1024]{2,1,0:T(8,128)(2,1)S(1)}, u32[]{:S(2)}, u32[]{:S(2)}) %all-to-all-start.2) | async-done | bytes 2097184 | tf_op jit(solution)/shard_map/all_to_all | solution.py:192
  276.7 1.5 gather_fusion.3
  278.3 1.3 pad_maximum_fusion
  279.6 3.6 %copy.45 = bf16[1792,2,256]{2,1,0:T(2,128)(2,1)} copy(bf16[1792,2,256]{0,2,1:T(8,128)(2,1)S(1)} %pad_maximum_fusion) | data formatting | bytes 3670016
  283.2 35.4 %all-gather.13.cloned.1.call-done = bf16[14,128,1024]{2,1,0:T(8,128)(2,1)} async-done(((bf16[14,32,1024]{2,1,0:T(8,128)(2,1)}), bf16[14,128,1024]{2,1,0:T(8,128)(2,1)}) %all-gather.13.cloned.1.call-update) | async-done | bytes 3670032 | tf_op jit(solution)/shard_map/all_gather | solution.py:194
  318.6 4.2 %copy.58 = bf16[1792,1024]{1,0:T(8,128)(2,1)} copy(bf16[1792,1024]{1,0:T(8,128)(2,1)} %bitcast.110) | data formatting | bytes 7340032
  (67 shorter events, 5.2 us)
Async XLA Ops:
  7.2 8.6 %copy-start.4 = (bf16[129,256]{1,0:T(8,128)(2,1)S(1)}, bf16[129,256]{1,0:T(8,128)(2,1)}, u32[]{:S(2)}) copy-start(bf16[129,256]{1,0:T(8,128)(2,1)} %constant.154.clone.1) | copy-start | bytes 198148
  7.2 58.2 %all-gather.7.cloned.1.call-start = ((), (), s32[]{:S(2)}) async-start(), calls=%async_computation.3 | async-start | bytes 1622016 | tf_op jit(solution)/shard_map/all_gather | solution.py:81
  8.6 103.3 %all-gather.9.cloned.1.call-start = ((), (), s32[]{:S(2)}) async-start(), calls=%async_computation.4 | async-start | bytes 4587520 | tf_op jit(solution)/shard_map/all_gather | solution.py:122
  15.7 1.6 copy-start.5
  15.7 1.6 copy-start.6
  15.7 1.6 copy-start.8
  58.2 1.4 copy-start
  65.4 129.1 %all-gather.11.cloned.1.call-start = ((), (), s32[]{:S(2)}) async-start(), calls=%async_computation.5 | async-start | bytes 19464192 | tf_op jit(solution)/shard_map/all_gather | solution.py:125
  113.3 4.6 %copy-start.7 = (s32[1,1,14,128]{3,1,2,0:T(1,128)}, s32[1,1,14,128]{3,1,2,0:T(1,128)S(1)}, u32[]{:S(2)}) copy-start(s32[1,1,14,128]{3,1,2,0:T(1,128)S(1)} %copy.54) | copy-start | bytes 21508
  122.9 5.2 %copy-start.1 = (bf16[1792,256]{0,1:T(8,128)(2,1)}, bf16[1792,256]{0,1:T(8,128)(2,1)S(1)}, u32[]{:S(2)}) copy-start(bf16[1792,256]{0,1:T(8,128)(2,1)S(1)} %convolution_convert_fusion.1) | copy-start | bytes 2752516
  128.1 40.3 %copy-start.3 = (bf16[1792,256]{0,1:T(8,128)(2,1)}, bf16[1792,256]{0,1:T(8,128)(2,1)S(1)}, u32[]{:S(2)}) copy-start(bf16[1792,256]{0,1:T(8,128)(2,1)S(1)} %convolution_convert_fusion) | copy-start | bytes 2752516
  179.4 14.6 %all-to-all-start.1 = ((bf16[14,4,32,256]{3,2,0,1:T(8,128)(2,1)}), bf16[14,4,32,256]{3,2,0,1:T(8,128)(2,1)S(1)}, u32[]{:S(2)}, u32[]{:S(2)}) async-start(bf16[14,4,32,256]{3,2,0,1:T(8,128)(2,1)} %copy.44), calls=%async_computation.1 | async-start | bytes 1835008 | tf_op jit(solution)/shard_map/all_to_all | solution.py:147
  198.9 2.5 copy-start.11
  198.9 2.5 copy-start.12
  231.3 3.7 %copy-start.9 = (f32[1024]{0:T(1024)S(1)}, f32[1024]{0:T(1024)}, u32[]{:S(2)}) copy-start(f32[1024]{0:T(1024)} %param.31) | copy-start | bytes 12292
  231.3 3.7 %copy-start.10 = (f32[1024]{0:T(1024)S(1)}, f32[1024]{0:T(1024)}, u32[]{:S(2)}) copy-start(f32[1024]{0:T(1024)} %param.30) | copy-start | bytes 12292
  237.6 40.7 %copy-start.2 = (bf16[1792,256]{0,1:T(8,128)(2,1)S(1)}, bf16[1792,256]{0,1:T(8,128)(2,1)}, u32[]{:S(2)}) copy-start(bf16[1792,256]{0,1:T(8,128)(2,1)} %copy-done.1) | copy-start | bytes 2752516
  237.6 39.1 %all-to-all-start.2 = ((bf16[32,32,1024]{2,1,0:T(8,128)(2,1)}), bf16[32,32,1024]{2,1,0:T(8,128)(2,1)S(1)}, u32[]{:S(2)}, u32[]{:S(2)}) async-start(bf16[32,32,1024]{2,1,0:T(8,128)(2,1)} %broadcast_select_fusion), calls=%async_computation.2 | async-start | bytes 4194304 | tf_op jit(solution)/shard_map/all_to_all | solution.py:192
  248.1 70.4 %all-gather.13.cloned.1.call-start = ((), (), s32[]{:S(2)}) async-start(), calls=%async_computation.6 | async-start | bytes 4587520 | tf_op jit(solution)/shard_map/all_gather | solution.py:194
Sparse Core Ops, SparseCore 0:
  10.2 55.0 all-gather.6
  67.6 44.2 all-gather.8
  114.1 80.2 all-gather.10
  278.4 40.1 all-gather.12
where the time goes:
time: 330 us; the launch traced here: 329 us
  waiting for transfers between devices  110 us (33%)
  blocking collectives  52.4 us (16%)
  matrix products  49.9 us (15%)
  Pallas kernels  38.5 us (12%)
  local copies, waits for them, and re-layouts  35.9 us (11%)
  starting transfers between devices  14.4 us (4%)
  between operations  14.3 us (4%)
  other arithmetic  14.2 us (4%)
    all_to_all x1, blocking collectives, body(): lax.all_to_all(send_pages, 'dp', split_axis=0, concat_axis=0, tiled=True)  40.9 us
    pallas_call x1, Pallas kernels, attention(): pl.pallas_call(_attn_kernel, out_shape=jax.ShapeDtypeStruct((heads, rows,...  38.5 us
    all_gather x1, waiting for transfers between devices, body(): lax.all_gather(mixed_mine, 'mp', axis=1).reshape(pages_dev * page, width)  35.4 us
    all_gather x1, waiting for transfers between devices, body(): lax.all_gather(dealt_part, 'mp', axis=2, tiled=True)  33.3 us
    all_to_all x1, waiting for transfers between devices, body(): lax.all_to_all(outgoing, 'dp', split_axis=0, concat_axis=0, tiled=True)  28.5 us
    dot_general x1, matrix products, body(): jnp.einsum('pid,du->piu', first_mine, full_up, preferred_element_type=jnp...  21.6 us
    dot_general x4, matrix products, body(): jnp.einsum('piu,ou->pio', hidden[:, :, group * unit_part:(group + 1) * un...  11.6 us
    all_gather x1, blocking collectives, body(): small_all = lax.all_gather(small, 'mp', axis=1)  11.5 us
  transfers between devices with their start and end apart: 6, of which 6 were waited for; matrix products, arithmetic and copies ran while one was open for 15% of the time, Pallas kernels for 12%

commit v1 on v0

--- a/solution.py
+++ b/solution.py
@@ -14,14 +14,18 @@
 
 
 def _attn_kernel(q_ref, k_ref, v_ref, qid_ref, kid_ref, o_ref):
-    scores = lax.dot_general(
-        q_ref[0], k_ref[0], (((1,), (1,)), ((), ())), preferred_element_type=jnp.float32
-    ) * (HEAD ** -0.5)
-    scores = jnp.where(qid_ref[...] == kid_ref[...], scores, -1e30)
-    highest = jnp.max(scores, axis=1, keepdims=True)
-    raised = jnp.exp(scores - highest)
-    weights = (raised / jnp.sum(raised, axis=1, keepdims=True)).astype(jnp.bfloat16)
-    o_ref[0] = jnp.dot(weights, v_ref[0], preferred_element_type=jnp.float32).astype(o_ref.dtype)
+    same = qid_ref[...] == kid_ref[...]
+    for head in range(q_ref.shape[0]):
+        scores = lax.dot_general(
+            q_ref[head], k_ref[head], (((1,), (1,)), ((), ())), preferred_element_type=jnp.float32
+        ) * (HEAD ** -0.5)
+        scores = jnp.where(same, scores, -1e30)
+        highest = jnp.max(scores, axis=1, keepdims=True)
+        raised = jnp.exp(scores - highest)
+        weights = (raised / jnp.sum(raised, axis=1, keepdims=True)).astype(jnp.bfloat16)
+        o_ref[:, head * HEAD : (head + 1) * HEAD] = jnp.dot(
+            weights, v_ref[head], preferred_element_type=jnp.float32
+        ).astype(o_ref.dtype)
 
 
 def attention(q, k, v, ids, block_q=256):
@@ -30,16 +34,16 @@
     kid = ids.reshape(1, rows)
     return pl.pallas_call(
         _attn_kernel,
-        out_shape=jax.ShapeDtypeStruct((heads, rows, dim), jnp.bfloat16),
-        grid=(heads, rows // block_q),
+        out_shape=jax.ShapeDtypeStruct((rows, heads * dim), jnp.bfloat16),
+        grid=(rows // block_q,),
         in_specs=[
-            pl.BlockSpec((1, block_q, dim), lambda h, i: (h, i, 0)),
-            pl.BlockSpec((1, rows, dim), lambda h, i: (h, 0, 0)),
-            pl.BlockSpec((1, rows, dim), lambda h, i: (h, 0, 0)),
-            pl.BlockSpec((block_q, 1), lambda h, i: (i, 0)),
-            pl.BlockSpec((1, rows), lambda h, i: (0, 0)),
+            pl.BlockSpec((heads, block_q, dim), lambda i: (0, i, 0)),
+            pl.BlockSpec((heads, rows, dim), lambda i: (0, 0, 0)),
+            pl.BlockSpec((heads, rows, dim), lambda i: (0, 0, 0)),
+            pl.BlockSpec((block_q, 1), lambda i: (i, 0)),
+            pl.BlockSpec((1, rows), lambda i: (0, 0)),
         ],
-        out_specs=pl.BlockSpec((1, block_q, dim), lambda h, i: (h, i, 0)),
+        out_specs=pl.BlockSpec((block_q, heads * dim), lambda i: (i, 0)),
         cost_estimate=pl.CostEstimate(
             flops=4 * heads * rows * rows * dim,
             transcendentals=heads * rows * rows,
@@ -94,32 +98,45 @@
     meta = meta.at[:, 0, :page].set(segment_ids.reshape(pages_dev, page).astype(tokens.dtype))
     meta = meta.at[:, 0, page].set(local_slot.astype(tokens.dtype))
     token_part = lax.dynamic_slice_in_dim(tokens, me_model * quarter, quarter, axis=1)
-    with_meta = jnp.concatenate([token_part.reshape(pages_dev, page, quarter), meta], axis=1)
-    send_pages = (
-        jnp.zeros((buffer_rows, page + 1, quarter), tokens.dtype)
-        .at[:, page, page]
+    token_pages = token_part.reshape(pages_dev, page, quarter)
+    half = page // 2
+    with_meta = jnp.concatenate([token_pages[:, :half], meta], axis=1)
+    send_first = (
+        jnp.zeros((buffer_rows, half + 1, quarter), tokens.dtype)
+        .at[:, half, page]
         .set(-1)
         .at[position]
         .set(with_meta)
     )
-    small, send_pages = lax.optimization_barrier((small, send_pages))
-    got_all = lax.all_to_all(send_pages, "dp", split_axis=0, concat_axis=0, tiled=True)
-    got_pages = got_all[:, :page]
-    got_ids = got_all[:, page, :page].astype(jnp.int32)
-    got_slots = got_all[:, page, page].astype(jnp.int32)
+    send_second = (
+        jnp.zeros((buffer_rows, page - half, quarter), tokens.dtype)
+        .at[position]
+        .set(token_pages[:, half:])
+    )
+    got_first = lax.all_to_all(send_first, "dp", split_axis=0, concat_axis=0, tiled=True)
+    got_ids = got_first[:, half, :page].astype(jnp.int32)
+    got_slots = got_first[:, half, page].astype(jnp.int32)
     matches = got_slots[None, :] == order[:, None]
     source_row = jnp.sum(
         jnp.where(matches, jnp.arange(buffer_rows, dtype=jnp.int32)[None, :], 0), axis=1
     )
+    dealt_first = got_first[:, :half][source_row]
+    dealt_first, attn_gathered = lax.optimization_barrier((dealt_first, attn_gathered))
+    dealt_first_all = lax.all_gather(dealt_first, "mp", axis=2, tiled=True)
+    send_second, dealt_first = lax.optimization_barrier((send_second, dealt_first))
+    got_second = lax.all_to_all(send_second, "dp", split_axis=0, concat_axis=0, tiled=True)
+    dealt_second = got_second[source_row]
+    small, dealt_second = lax.optimization_barrier((small, dealt_second))
+    dealt_second_all = lax.all_gather(dealt_second, "mp", axis=2, tiled=True)
     small_all = lax.all_gather(small, "mp", axis=1)
     rows_dp = small.shape[0]
     out_rows = small_all[:, :, :in_part].reshape(rows_dp, n_model * in_part)
     up_rows = small_all[:, :, in_part : in_part + unit_part].reshape(rows_dp, n_model * unit_part)
     down_rows = small_all[:, :, in_part + unit_part :].reshape(rows_dp, n_model * unit_part)
     ffn_local = jnp.concatenate([out_rows, up_rows, down_rows], axis=1)
-    dealt_part = got_pages[source_row]
-    dealt_part, attn_gathered = lax.optimization_barrier((dealt_part, attn_gathered))
-    dealt = lax.all_gather(dealt_part, "mp", axis=2, tiled=True).reshape(pages_dev * page, width)
+    dealt = jnp.concatenate([dealt_first_all, dealt_second_all], axis=1).reshape(
+        pages_dev * page, width
+    )
     dealt_ids = got_ids[source_row].reshape(pages_dev * page)
     ffn_local, dealt = lax.optimization_barrier((ffn_local, dealt))
     ffn_gathered = lax.all_gather(ffn_local, "dp", axis=0, tiled=True)
@@ -138,11 +155,7 @@
     def by_head(x):
         return x.reshape(rows, heads_here, HEAD).transpose(1, 0, 2)
 
-    context = (
-        attention(by_head(query), by_head(keys), by_head(values), dealt_ids)
-        .transpose(1, 0, 2)
-        .reshape(rows, heads_here * HEAD)
-    )
+    context = attention(by_head(query), by_head(keys), by_head(values), dealt_ids)
 
     context_rows = lax.all_to_all(
         context.reshape(pages_dev, n_model, sub, head_cols),
@@ -189,9 +202,12 @@
         second_mine[jnp.clip(got_slots, 0, pages_dev - 1)],
         jnp.zeros((), second_mine.dtype),
     )
-    returned = lax.all_to_all(outgoing, "dp", split_axis=0, concat_axis=0, tiled=True)
-    mixed_mine = returned[position]
-    mixed = lax.all_gather(mixed_mine, "mp", axis=1).reshape(pages_dev * page, width)
+    piece = sub // 2
+    back_first = lax.all_to_all(outgoing[:, :piece], "dp", split_axis=0, concat_axis=0, tiled=True)
+    back_second = lax.all_to_all(outgoing[:, piece:], "dp", split_axis=0, concat_axis=0, tiled=True)
+    mixed_first = lax.all_gather(back_first[position], "mp", axis=1)
+    mixed_second = lax.all_gather(back_second[position], "mp", axis=1)
+    mixed = jnp.concatenate([mixed_first, mixed_second], axis=2).reshape(pages_dev * page, width)
     kv_cache = jnp.stack([keys, values], axis=1)
     return (mixed, kv_cache)
 

time: 330 us -> 356 us (1.079)
  waiting for transfers between devices: 110 us -> 130 us
  blocking collectives: 52.4 us -> 61.6 us
  other arithmetic: 14.2 us -> 20.1 us
  Pallas kernels: 38.5 us -> 33 us
  local copies, waits for them, and re-layouts: 35.9 us -> 31.1 us
    all_gather x1, waiting for transfers between devices: 0.39 us -> 13.1 us  [body(): ffn_gathered = lax.all_gather(ffn_local, 'dp', axis=0, tiled=True)]
    all_gather x1, waiting for transfers between devices: 2.85 us -> 15.1 us  [body(): attn_gathered = lax.all_gather(attn_local, 'dp', axis=0, tiled=True)]
    all_gather x2 -> x4, waiting for transfers between devices: 68.6 us -> 57.2 us  [the longest x1 29 us: body(): dealt_second_all = lax.all_gather(dealt_second, 'mp', axis=2, tiled=True)]
    concatenate x1 -> x3, other arithmetic: 0.08 us -> 8.94 us  [the longest x1 4.57 us: body(): jnp.concatenate([mixed_first, mixed_second], axis=2)]
    transpose x1 -> x0, local copies, waits for them, and re-layouts: 8.78 us -> none  [body(): context = attention(by_head(query), by_head(keys), by_head(values), dealt...]
    all_to_all x1 -> x2, blocking collectives: 40.9 us -> 49.6 us  [the longest x1 28.7 us: body(): lax.all_to_all(send_first, 'dp', split_axis=0, concat_axis=0, tiled=True)]
    pallas_call x1, Pallas kernels: 38.5 us -> 33 us  [attention(): pl.pallas_call(_attn_kernel, out_shape=jax.ShapeDtypeStruct((rows, heads...]
    all_to_all x1 -> x2, waiting for transfers between devices: 28.5 us -> 34 us  [the longest x1 17 us: body(): lax.all_to_all(outgoing[:, :piece], 'dp', split_axis=0, concat_axis=0, ti...]
  transfers between devices with their start and end apart: 6 -> 9, of which waited for: 6 -> 7; matrix products, arithmetic and copies ran while one was open for 15% -> 13% of each run, Pallas kernels for 12% -> 9%
where the time goes in v1:
time: 356 us; the launch traced here: 355 us
  waiting for transfers between devices  130 us (37%)
  blocking collectives  61.6 us (17%)
  matrix products  49.9 us (14%)
  Pallas kernels  33 us (9%)
  local copies, waits for them, and re-layouts  31.1 us (9%)
  other arithmetic  20.1 us (6%)
  starting transfers between devices  14.8 us (4%)
  between operations  14.6 us (4%)
    pallas_call x1, Pallas kernels, attention(): pl.pallas_call(_attn_kernel, out_shape=jax.ShapeDtypeStruct((rows, heads...  33 us
    all_gather x1, waiting for transfers between devices, body(): dealt_second_all = lax.all_gather(dealt_second, 'mp', axis=2, tiled=True)  29 us
    all_to_all x1, blocking collectives, body(): lax.all_to_all(send_first, 'dp', split_axis=0, concat_axis=0, tiled=True)  28.7 us
    all_gather x1, waiting for transfers between devices, body(): mixed_second = lax.all_gather(back_second[position], 'mp', axis=1)  28.2 us
    dot_general x1, matrix products, body(): jnp.einsum('pid,du->piu', first_mine, full_up, preferred_element_type=jnp...  21.6 us
    all_to_all x1, blocking collectives, body(): lax.all_to_all(outgoing[:, piece:], 'dp', split_axis=0, concat_axis=0, ti...  20.9 us
    all_to_all x1, waiting for transfers between devices, body(): lax.all_to_all(outgoing[:, :piece], 'dp', split_axis=0, concat_axis=0, ti...  17 us
    all_to_all x1, waiting for transfers between devices, body(): lax.all_to_all(send_second, 'dp', split_axis=0, concat_axis=0, tiled=True)  16.9 us
  transfers between devices with their start and end apart: 9, of which 7 were waited for; matrix products, arithmetic and copies ran while one was open for 13% of the time, Pallas kernels for 9%

profile of v1, /device:TPU:1, one launch (start us, length us, event | category | flops | bytes accessed | tf_op | source)
XLA Modules:
  0.0 355.1 jit_solution(13476552302743676895)
XLA Ops:
  7.2 1.5 pad_maximum_fusion.6
  10.9 1.4 and_reduce_fusion
  12.3 1.4 broadcast_select_fusion.1
  14.5 1.2 constant_dynamic-slice_fusion
  15.9 1.3 scatter_fusion
  17.2 28.7 %all_to_all.25 = bf16[32,65,256]{2,1,0:T(8,128)(2,1)S(1)} all-to-all(bf16[32,65,256]{2,1,0:T(8,128)(2,1)S(1)} %scatter_fusion), channel_id=1, replica_groups=mesh['dp'=32,'mp'=4] {'dp'}, dimensions={0} | all-to-all | bytes 2129920 | tf_op jit(solution)/shard_map/all_to_all | solution.py:116
  46.1 1.2 clamp_reduce_fusion
  47.5 1.3 gather_fusion
  48.8 15.1 %all-gather.10.cloned.1.call-done = bf16[1024,768]{1,0:T(8,128)(2,1)} async-done(((bf16[32,768]{1,0:T(8,128)(2,1)}), bf16[1024,768]{1,0:T(8,128)(2,1)}) %all-gather.10.cloned.1.call-update) | async-done | bytes 1572880 | tf_op jit(solution)/shard_map/all_gather | solution.py:85
  64.0 1.1 broadcast_in_dim.29
  65.1 2.5 scatter_fusion.1
  67.6 5.2 %all-to-all-start.1 = ((bf16[32,64,256]{2,1,0:T(8,128)(2,1)}), bf16[32,64,256]{2,1,0:T(8,128)(2,1)S(1)}, u32[]{:S(2)}, u32[]{:S(2)}) async-start(bf16[32,64,256]{2,1,0:T(8,128)(2,1)} %scatter_fusion.1), calls=%async_computation.1 | async-start | bytes 2097152 | tf_op jit(solution)/shard_map/all_to_all | solution.py:127
  72.9 16.9 %all-to-all-done.1 = bf16[32,64,256]{2,1,0:T(8,128)(2,1)S(1)} async-done(((bf16[32,64,256]{2,1,0:T(8,128)(2,1)}), bf16[32,64,256]{2,1,0:T(8,128)(2,1)S(1)}, u32[]{:S(2)}, u32[]{:S(2)}) %all-to-all-start.1) | async-done | bytes 1048608 | tf_op jit(solution)/shard_map/all_to_all | solution.py:127
  89.8 1.3 gather_fusion.1
  91.3 12.0 %all-gather = bf16[32,9216]{1,0:T(8,128)(2,1)S(1)} all-gather(bf16[32,2304]{1,0:T(8,128)(2,1)S(1)} %pad_maximum_fusion.5), channel_id=2, replica_groups=mesh['dp'=32,'mp'=4] {'mp'}, dimensions={1}, use_global_device_ids=true | all-gather | bytes 737280 | tf_op jit(solution)/shard_map/all_gather | solution.py:131
  104.9 29.0 %all-gather.14.cloned.1.call-done = bf16[14,64,1024]{2,1,0:T(8,128)(2,1)} async-done(((bf16[14,64,256]{2,1,0:T(8,128)(2,1)}), bf16[14,64,1024]{2,1,0:T(8,128)(2,1)}) %all-gather.14.cloned.1.call-update) | async-done | bytes 1835024 | tf_op jit(solution)/shard_map/all_gather | solution.py:130
  134.0 4.3 %pad_maximum_fusion = bf16[14,128,1024]{2,1,0:T(8,128)(2,1)} fusion(bf16[14,64,1024]{2,1,0:T(8,128)(2,1)} %all-gather.14.cloned.1.call-done, bf16[14,64,1024]{2,1,0:T(8,128)(2,1)} %all-gather.12.cloned.1.call-done), kind=kLoop, calls=%fused_computation.29 | loop fusion | flops 7340032 | bytes 7340032 | tf_op jit(solution)/shard_map/concatenate | solution.py:137
  138.9 1.3 copy.49
  140.3 3.3 convolution_convert_fusion.2
  143.6 1.6 copy.38
  145.2 3.3 convolution_convert_fusion.1
  148.5 1.6 copy.39
  150.2 3.6 %convolution_convert_fusion = bf16[1792,256]{0,1:T(8,128)(2,1)S(1)} fusion(bf16[1792,1024]{1,0:T(8,128)(2,1)} %bitcast.115, bf16[1024,768]{1,0:T(8,128)(2,1)} %all-gather.10.cloned.1.call-done), kind=kOutput, calls=%fused_computation.31 | convolution fusion | flops 939982848 | bytes 5111808 | tf_op jit(solution)/shard_map/dot_general | solution.py:151
  153.8 1.7 copy.40
  155.4 33.0 %shard_map.140 = bf16[1792,256]{1,0:T(8,128)(2,1)} custom-call(bf16[4,1792,64]{2,1,0:T(8,128)(2,1)} %bitcast.125, bf16[4,1792,64]{2,1,0:T(8,128)(2,1)} %bitcast.126, bf16[4,1792,64]{2,1,0:T(8,128)(2,1)} %bitcast.127, s32[1792,1]{1,0:T(8,128)} %bitcast.133, s32[1,1792]{1,0:T(1,128)} %bitcast.141), custom_call_target="tpu_custom_call" | custom-call | flops 3288334336 | bytes 3670016 | tf_op jit(solution)/shard_map/pallas_call | solution.py:35
  188.4 2.2 copy.42
  190.6 3.7 %all-to-all-start.2 = ((bf16[14,4,32,256]{3,2,0,1:T(8,128)(2,1)}), bf16[14,4,32,256]{3,2,0,1:T(8,128)(2,1)S(1)}, u32[]{:S(2)}, u32[]{:S(2)}) async-start(bf16[14,4,32,256]{3,2,0,1:T(8,128)(2,1)} %copy.42), calls=%async_computation.2 | async-start | bytes 1835008 | tf_op jit(solution)/shard_map/all_to_all | solution.py:160
  195.1 10.6 %all-to-all-done.2 = bf16[14,4,32,256]{3,2,0,1:T(8,128)(2,1)S(1)} async-done(((bf16[14,4,32,256]{3,2,0,1:T(8,128)(2,1)}), bf16[14,4,32,256]{3,2,0,1:T(8,128)(2,1)S(1)}, u32[]{:S(2)}, u32[]{:S(2)}) %all-to-all-start.2) | async-done | bytes 917536 | tf_op jit(solution)/shard_map/all_to_all | solution.py:160
  205.7 13.1 %all-gather.16.cloned.1.call-done = bf16[1024,9216]{1,0:T(8,128)(2,1)} async-done(((bf16[32,9216]{1,0:T(8,128)(2,1)}), bf16[1024,9216]{1,0:T(8,128)(2,1)}) %all-gather.16.cloned.1.call-update) | async-done | bytes 18874384 | tf_op jit(solution)/shard_map/all_gather | solution.py:142
  218.7 1.5 convolution_convert_fusion.4
  220.2 1.5 convolution_convert_fusion.5
  221.7 1.5 convolution_convert_fusion.6
  223.2 2.2 fusion.35
  225.7 21.6 %fusion.3 = bf16[14,32,4096]{2,1,0:T(8,128)(2,1)S(1)} fusion(bf16[1024,9216]{1,0:T(8,128)(2,1)} %all-gather.16.cloned.1.call-done, f32[14,32,1024]{2,1,0:T(8,128)S(1)} %get-tuple-element.69, f32[1024]{0:T(1024)S(1)} %copy-done.10, f32[1024]{0:T(1024)S(1)} %copy-done.11, f32[14,32]{1,0:T(8,128)S(1)} %add_rsqrt_fusion.1, ...), kind=kOutput, calls=%fused_computation.13 | convolution fusion | flops 3879665664 | bytes 13905408 | tf_op jit(solution)/shard_map/pid,du->piu/dot_general | solution.py:183
  247.3 2.7 fusion.17
  250.1 2.7 fusion.16
  252.8 2.7 fusion.15
  255.6 3.3 fusion.36
  260.6 1.2 fusion.32
  261.7 5.6 %all-to-all-start.3 = ((bf16[32,16,1024]{2,1,0:T(8,128)(2,1)}), bf16[32,16,1024]{2,1,0:T(8,128)(2,1)}, u32[]{:S(2)}, u32[]{:S(2)}) async-start(bf16[32,16,1024]{2,1,0:T(8,128)(2,1)} %get-tuple-element.60), calls=%async_computation.3 | async-start | bytes 2097152 | tf_op jit(solution)/shard_map/all_to_all | solution.py:206
  267.4 17.0 %all-to-all-done.3 = bf16[32,16,1024]{2,1,0:T(8,128)(2,1)} async-done(((bf16[32,16,1024]{2,1,0:T(8,128)(2,1)}), bf16[32,16,1024]{2,1,0:T(8,128)(2,1)}, u32[]{:S(2)}, u32[]{:S(2)}) %all-to-all-start.3) | async-done | bytes 1048608 | tf_op jit(solution)/shard_map/all_to_all | solution.py:206
  284.4 2.6 gather_fusion.4
  287.1 20.9 %all_to_all.26 = bf16[32,16,1024]{2,1,0:T(8,128)(2,1)} all-to-all(bf16[32,16,1024]{2,1,0:T(8,128)(2,1)S(1)} %get-tuple-element.61), channel_id=1, replica_groups=mesh['dp'=32,'mp'=4] {'dp'}, dimensions={0} | all-to-all | bytes 2097152 | tf_op jit(solution)/shard_map/all_to_all | solution.py:207
  308.0 2.6 gather_fusion.5
  310.6 1.3 pad_maximum_fusion.2
  311.9 3.6 %copy.43 = bf16[1792,2,256]{2,1,0:T(2,128)(2,1)} copy(bf16[1792,2,256]{0,2,1:T(8,128)(2,1)S(1)} %pad_maximum_fusion.2) | data formatting | bytes 3670016
  315.5 28.2 %all-gather.20.cloned.1.call-done = bf16[14,64,1024]{2,1,0:T(8,128)(2,1)} async-done(((bf16[14,16,1024]{2,1,0:T(8,128)(2,1)}), bf16[14,64,1024]{2,1,0:T(8,128)(2,1)}) %all-gather.20.cloned.1.call-update) | async-done | bytes 1835024 | tf_op jit(solution)/shard_map/all_gather | solution.py:209
  343.7 4.6 %pad_maximum_fusion.1 = bf16[14,4,32,1024]{3,2,1,0:T(8,128)(2,1)} fusion(bf16[14,4,16,1024]{3,2,1,0:T(8,128)(2,1)} %bitcast.124, bf16[14,4,16,1024]{3,2,1,0:T(8,128)(2,1)} %bitcast.123), kind=kLoop, calls=%fused_computation.30 | loop fusion | flops 7340032 | bytes 7340032 | tf_op jit(solution)/shard_map/concatenate | solution.py:210
  (78 shorter events, 8.6 us)
Async XLA Ops:
  7.2 8.7 %copy-start = (bf16[32,65,256]{2,1,0:T(8,128)(2,1)S(1)}, bf16[32,65,256]{2,1,0:T(8,128)(2,1)}, u32[]{:S(2)}) copy-start(bf16[32,65,256]{2,1,0:T(8,128)(2,1)} %constant.156.clone.1) | copy-start | bytes 3194884
  7.2 56.8 %all-gather.10.cloned.1.call-start = ((), (), s32[]{:S(2)}) async-start(), calls=%async_computation.5 | async-start | bytes 1622016 | tf_op jit(solution)/shard_map/all_gather | solution.py:85
  8.7 96.2 %all-gather.12.cloned.1.call-start = ((), (), s32[]{:S(2)}) async-start(), calls=%async_computation.6 | async-start | bytes 2293760 | tf_op jit(solution)/shard_map/all_gather | solution.py:125
  46.0 26.9 %copy-start.4 = (bf16[1024,32]{0,1:T(8,128)(2,1)S(1)}, bf16[1024,32]{0,1:T(8,128)(2,1)}, u32[]{:S(2)}) copy-start(bf16[1024,32]{0,1:T(8,128)(2,1)} %param.27) | copy-start | bytes 196612
  46.0 26.9 %copy-start.5 = (bf16[32,1024]{1,0:T(8,128)(2,1)S(1)}, bf16[32,1024]{1,0:T(8,128)(2,1)}, u32[]{:S(2)}) copy-start(bf16[32,1024]{1,0:T(8,128)(2,1)} %param.26) | copy-start | bytes 196612
  46.0 26.9 %copy-start.7 = (bf16[256,32]{0,1:T(8,128)(2,1)S(1)}, bf16[256,32]{0,1:T(8,128)(2,1)}, u32[]{:S(2)}) copy-start(bf16[256,32]{0,1:T(8,128)(2,1)} %param.25) | copy-start | bytes 49156
  67.6 22.3 %all-to-all-start.1 = ((bf16[32,64,256]{2,1,0:T(8,128)(2,1)}), bf16[32,64,256]{2,1,0:T(8,128)(2,1)S(1)}, u32[]{:S(2)}, u32[]{:S(2)}) async-start(bf16[32,64,256]{2,1,0:T(8,128)(2,1)} %scatter_fusion.1), calls=%async_computation.1 | async-start | bytes 2097152 | tf_op jit(solution)/shard_map/all_to_all | solution.py:127
  72.8 61.2 %all-gather.14.cloned.1.call-start = ((), (), s32[]{:S(2)}) async-start(), calls=%async_computation.7 | async-start | bytes 2293760 | tf_op jit(solution)/shard_map/all_gather | solution.py:130
  91.2 127.5 %all-gather.16.cloned.1.call-start = ((), (), s32[]{:S(2)}) async-start(), calls=%async_computation.8 | async-start | bytes 19464192 | tf_op jit(solution)/shard_map/all_gather | solution.py:142
  138.9 4.7 %copy-start.6 = (s32[1,1,14,128]{3,1,2,0:T(1,128)}, s32[1,1,14,128]{3,1,2,0:T(1,128)S(1)}, u32[]{:S(2)}) copy-start(s32[1,1,14,128]{3,1,2,0:T(1,128)S(1)} %copy.52) | copy-start | bytes 21508
  148.5 5.2 %copy-start.1 = (bf16[1792,256]{0,1:T(8,128)(2,1)}, bf16[1792,256]{0,1:T(8,128)(2,1)S(1)}, u32[]{:S(2)}) copy-start(bf16[1792,256]{0,1:T(8,128)(2,1)S(1)} %convolution_convert_fusion.1) | copy-start | bytes 2752516
  153.8 34.6 %copy-start.3 = (bf16[1792,256]{0,1:T(8,128)(2,1)}, bf16[1792,256]{0,1:T(8,128)(2,1)S(1)}, u32[]{:S(2)}) copy-start(bf16[1792,256]{0,1:T(8,128)(2,1)S(1)} %convolution_convert_fusion) | copy-start | bytes 2752516
  190.6 15.0 %all-to-all-start.2 = ((bf16[14,4,32,256]{3,2,0,1:T(8,128)(2,1)}), bf16[14,4,32,256]{3,2,0,1:T(8,128)(2,1)S(1)}, u32[]{:S(2)}, u32[]{:S(2)}) async-start(bf16[14,4,32,256]{3,2,0,1:T(8,128)(2,1)} %copy.42), calls=%async_computation.2 | async-start | bytes 1835008 | tf_op jit(solution)/shard_map/all_to_all | solution.py:160
  223.2 2.5 copy-start.10
  223.2 2.5 copy-start.11
  255.6 3.7 %copy-start.8 = (f32[1024]{0:T(1024)S(1)}, f32[1024]{0:T(1024)}, u32[]{:S(2)}) copy-start(f32[1024]{0:T(1024)} %param.31) | copy-start | bytes 12292
  255.6 3.7 %copy-start.9 = (f32[1024]{0:T(1024)S(1)}, f32[1024]{0:T(1024)}, u32[]{:S(2)}) copy-start(f32[1024]{0:T(1024)} %param.30) | copy-start | bytes 12292
  261.7 48.8 %copy-start.2 = (bf16[1792,256]{0,1:T(8,128)(2,1)S(1)}, bf16[1792,256]{0,1:T(8,128)(2,1)}, u32[]{:S(2)}) copy-start(bf16[1792,256]{0,1:T(8,128)(2,1)} %copy-done.1) | copy-start | bytes 2752516
  261.7 22.7 %all-to-all-start.3 = ((bf16[32,16,1024]{2,1,0:T(8,128)(2,1)}), bf16[32,16,1024]{2,1,0:T(8,128)(2,1)}, u32[]{:S(2)}, u32[]{:S(2)}) async-start(bf16[32,16,1024]{2,1,0:T(8,128)(2,1)} %get-tuple-element.60), calls=%async_computation.3 | async-start | bytes 2097152 | tf_op jit(solution)/shard_map/all_to_all | solution.py:206
  267.3 48.2 %all-gather.18.cloned.1.call-start = ((), (), s32[]{:S(2)}) async-start(), calls=%async_computation.9 | async-start | bytes 2293760 | tf_op jit(solution)/shard_map/all_gather | solution.py:208
  287.0 56.7 %all-gather.20.cloned.1.call-start = ((), (), s32[]{:S(2)}) async-start(), calls=%async_computation.10 | async-start | bytes 2293760 | tf_op jit(solution)/shard_map/all_gather | solution.py:209
Sparse Core Ops, SparseCore 0:
  10.8 53.1 all-gather.9
  66.2 29.1 all-gather.11
  97.6 36.2 all-gather.13
  138.4 80.2 all-gather.15
  287.2 25.8 all-gather.17
  315.1 28.5 all-gather.19

commit v2 on v0

--- a/solution.py
+++ b/solution.py
@@ -14,14 +14,18 @@
 
 
 def _attn_kernel(q_ref, k_ref, v_ref, qid_ref, kid_ref, o_ref):
-    scores = lax.dot_general(
-        q_ref[0], k_ref[0], (((1,), (1,)), ((), ())), preferred_element_type=jnp.float32
-    ) * (HEAD ** -0.5)
-    scores = jnp.where(qid_ref[...] == kid_ref[...], scores, -1e30)
-    highest = jnp.max(scores, axis=1, keepdims=True)
-    raised = jnp.exp(scores - highest)
-    weights = (raised / jnp.sum(raised, axis=1, keepdims=True)).astype(jnp.bfloat16)
-    o_ref[0] = jnp.dot(weights, v_ref[0], preferred_element_type=jnp.float32).astype(o_ref.dtype)
+    same = qid_ref[...] == kid_ref[...]
+    for head in range(q_ref.shape[0]):
+        scores = lax.dot_general(
+            q_ref[head], k_ref[head], (((1,), (1,)), ((), ())), preferred_element_type=jnp.float32
+        ) * (HEAD ** -0.5)
+        scores = jnp.where(same, scores, -1e30)
+        highest = jnp.max(scores, axis=1, keepdims=True)
+        raised = jnp.exp(scores - highest)
+        weights = (raised / jnp.sum(raised, axis=1, keepdims=True)).astype(jnp.bfloat16)
+        o_ref[:, head * HEAD : (head + 1) * HEAD] = jnp.dot(
+            weights, v_ref[head], preferred_element_type=jnp.float32
+        ).astype(o_ref.dtype)
 
 
 def attention(q, k, v, ids, block_q=256):
@@ -30,16 +34,16 @@
     kid = ids.reshape(1, rows)
     return pl.pallas_call(
         _attn_kernel,
-        out_shape=jax.ShapeDtypeStruct((heads, rows, dim), jnp.bfloat16),
-        grid=(heads, rows // block_q),
+        out_shape=jax.ShapeDtypeStruct((rows, heads * dim), jnp.bfloat16),
+        grid=(rows // block_q,),
         in_specs=[
-            pl.BlockSpec((1, block_q, dim), lambda h, i: (h, i, 0)),
-            pl.BlockSpec((1, rows, dim), lambda h, i: (h, 0, 0)),
-            pl.BlockSpec((1, rows, dim), lambda h, i: (h, 0, 0)),
-            pl.BlockSpec((block_q, 1), lambda h, i: (i, 0)),
-            pl.BlockSpec((1, rows), lambda h, i: (0, 0)),
+            pl.BlockSpec((heads, block_q, dim), lambda i: (0, i, 0)),
+            pl.BlockSpec((heads, rows, dim), lambda i: (0, 0, 0)),
+            pl.BlockSpec((heads, rows, dim), lambda i: (0, 0, 0)),
+            pl.BlockSpec((block_q, 1), lambda i: (i, 0)),
+            pl.BlockSpec((1, rows), lambda i: (0, 0)),
         ],
-        out_specs=pl.BlockSpec((1, block_q, dim), lambda h, i: (h, i, 0)),
+        out_specs=pl.BlockSpec((block_q, heads * dim), lambda i: (i, 0)),
         cost_estimate=pl.CostEstimate(
             flops=4 * heads * rows * rows * dim,
             transcendentals=heads * rows * rows,
@@ -138,11 +142,7 @@
     def by_head(x):
         return x.reshape(rows, heads_here, HEAD).transpose(1, 0, 2)
 
-    context = (
-        attention(by_head(query), by_head(keys), by_head(values), dealt_ids)
-        .transpose(1, 0, 2)
-        .reshape(rows, heads_here * HEAD)
-    )
+    context = attention(by_head(query), by_head(keys), by_head(values), dealt_ids)
 
     context_rows = lax.all_to_all(
         context.reshape(pages_dev, n_model, sub, head_cols),

time: 330 us -> 327 us (level)
  waiting for transfers between devices: 110 us -> 126 us
  local copies, waits for them, and re-layouts: 35.9 us -> 27 us
  Pallas kernels: 38.5 us -> 32.9 us
  starting transfers between devices: 14.4 us -> 9.53 us
    all_gather x1, waiting for transfers between devices: 0.39 us -> 14.9 us  [body(): ffn_gathered = lax.all_gather(ffn_local, 'dp', axis=0, tiled=True)]
    transpose x1 -> x0, local copies, waits for them, and re-layouts: 8.78 us -> none  [body(): context = attention(by_head(query), by_head(keys), by_head(values), dealt...]
    pallas_call x1, Pallas kernels: 38.5 us -> 32.9 us  [attention(): pl.pallas_call(_attn_kernel, out_shape=jax.ShapeDtypeStruct((rows, heads...]
    all_to_all x1, starting transfers between devices: 10.5 us -> 5.54 us  [body(): lax.all_to_all(outgoing, 'dp', split_axis=0, concat_axis=0, tiled=True)]
  transfers between devices with their start and end apart: 6 -> 6, of which waited for: 6 -> 6; matrix products, arithmetic and copies ran while one was open for 15% -> 12% of each run, Pallas kernels for 12% -> 10%
where the time goes in v2:
time: 327 us; the launch traced here: 326 us
  waiting for transfers between devices  126 us (39%)
  blocking collectives  52.4 us (16%)
  matrix products  49.9 us (15%)
  Pallas kernels  32.9 us (10%)
  local copies, waits for them, and re-layouts  27 us (8%)
  between operations  14.3 us (4%)
  other arithmetic  14.2 us (4%)
  starting transfers between devices  9.53 us (3%)
    all_to_all x1, blocking collectives, body(): lax.all_to_all(send_pages, 'dp', split_axis=0, concat_axis=0, tiled=True)  40.9 us
    all_gather x1, waiting for transfers between devices, body(): lax.all_gather(mixed_mine, 'mp', axis=1).reshape(pages_dev * page, width)  37.2 us
    all_gather x1, waiting for transfers between devices, body(): lax.all_gather(dealt_part, 'mp', axis=2, tiled=True)  33.2 us
    pallas_call x1, Pallas kernels, attention(): pl.pallas_call(_attn_kernel, out_shape=jax.ShapeDtypeStruct((rows, heads...  32.9 us
    all_to_all x1, waiting for transfers between devices, body(): lax.all_to_all(outgoing, 'dp', split_axis=0, concat_axis=0, tiled=True)  28.5 us
    dot_general x1, matrix products, body(): jnp.einsum('pid,du->piu', first_mine, full_up, preferred_element_type=jnp...  21.6 us
    all_gather x1, waiting for transfers between devices, body(): ffn_gathered = lax.all_gather(ffn_local, 'dp', axis=0, tiled=True)  14.9 us
    dot_general x4, matrix products, body(): jnp.einsum('piu,ou->pio', hidden[:, :, group * unit_part:(group + 1) * un...  11.6 us
  transfers between devices with their start and end apart: 6, of which 6 were waited for; matrix products, arithmetic and copies ran while one was open for 12% of the time, Pallas kernels for 10%

profile of v2, /device:TPU:1, one launch (start us, length us, event | category | flops | bytes accessed | tf_op | source)
XLA Modules:
  0.0 326.2 jit_solution(6737277010002309362)
XLA Ops:
  7.2 1.4 pad_maximum_fusion.4
  9.3 0.7 fusion.29
  10.0 0.7 convert_bitcast_fusion
  10.9 1.4 and_reduce_fusion
  12.2 1.4 broadcast_select_fusion.1
  13.6 0.8 scatter.24
  14.4 1.2 constant_dynamic-slice_fusion
  15.9 1.3 scatter_fusion
  17.3 40.9 %all_to_all.15 = bf16[32,129,256]{2,1,0:T(8,128)(2,1)S(1)} all-to-all(bf16[32,129,256]{2,1,0:T(8,128)(2,1)S(1)} %scatter_fusion), channel_id=1, replica_groups=mesh['dp'=32,'mp'=4] {'dp'}, dimensions={0} | all-to-all | bytes 4227072 | tf_op jit(solution)/shard_map/all_to_all | solution.py:110
  58.5 1.1 copy-done
  59.6 1.2 clamp_reduce_fusion
  60.9 1.5 gather_fusion
  62.5 2.9 all-gather.7.cloned.1.call-done
  65.4 11.5 %all-gather = bf16[32,9216]{1,0:T(8,128)(2,1)S(1)} all-gather(bf16[32,2304]{1,0:T(8,128)(2,1)S(1)} %pad_maximum_fusion.3), channel_id=2, replica_groups=mesh['dp'=32,'mp'=4] {'mp'}, dimensions={1}, use_global_device_ids=true | all-gather | bytes 737280 | tf_op jit(solution)/shard_map/all_gather | solution.py:118
  77.8 0.9 pad_maximum_fusion.2
  78.7 33.2 %all-gather.9.cloned.1.call-done = bf16[14,128,1024]{2,1,0:T(8,128)(2,1)} async-done(((bf16[14,128,256]{2,1,0:T(8,128)(2,1)}), bf16[14,128,1024]{2,1,0:T(8,128)(2,1)}) %all-gather.9.cloned.1.call-update) | async-done | bytes 3670032 | tf_op jit(solution)/shard_map/all_gather | solution.py:126
  111.9 0.9 slice_convert_fusion
  113.4 1.3 copy.49
  114.6 3.3 %convolution_convert_fusion.2 = bf16[1792,256]{0,1:T(8,128)(2,1)S(1)} fusion(bf16[1792,1024]{1,0:T(8,128)(2,1)} %bitcast.129, bf16[1024,768]{1,0:T(8,128)(2,1)} %all-gather.7.cloned.1.call-done), kind=kOutput, calls=%fused_computation.28 | convolution fusion | flops 939982848 | bytes 5111808 | tf_op jit(solution)/shard_map/dot_general | solution.py:136
  117.9 1.6 copy.38
  119.6 3.3 %convolution_convert_fusion.1 = bf16[1792,256]{0,1:T(8,128)(2,1)S(1)} fusion(bf16[1792,1024]{1,0:T(8,128)(2,1)} %bitcast.130, bf16[1024,768]{1,0:T(8,128)(2,1)} %all-gather.7.cloned.1.call-done), kind=kOutput, calls=%fused_computation.27 | convolution fusion | flops 939982848 | bytes 5111808 | tf_op jit(solution)/shard_map/dot_general | solution.py:137
  122.9 1.6 copy.39
  124.6 3.5 %convolution_convert_fusion = bf16[1792,256]{0,1:T(8,128)(2,1)S(1)} fusion(bf16[1792,1024]{1,0:T(8,128)(2,1)} %bitcast.131, bf16[1024,768]{1,0:T(8,128)(2,1)} %all-gather.7.cloned.1.call-done), kind=kOutput, calls=%fused_computation.26 | convolution fusion | flops 939982848 | bytes 5111808 | tf_op jit(solution)/shard_map/dot_general | solution.py:138
  128.1 1.7 copy.40
  129.8 32.9 %shard_map.140 = bf16[1792,256]{1,0:T(8,128)(2,1)} custom-call(bf16[4,1792,64]{2,1,0:T(8,128)(2,1)} %bitcast.116, bf16[4,1792,64]{2,1,0:T(8,128)(2,1)} %bitcast.117, bf16[4,1792,64]{2,1,0:T(8,128)(2,1)} %bitcast.118, s32[1792,1]{1,0:T(8,128)} %bitcast.124, s32[1,1792]{1,0:T(1,128)} %bitcast.136), custom_call_target="tpu_custom_call" | custom-call | flops 3288334336 | bytes 3670016 | tf_op jit(solution)/shard_map/pallas_call | solution.py:35
  162.8 2.2 copy.42
  164.9 3.8 %all-to-all-start.1 = ((bf16[14,4,32,256]{3,2,0,1:T(8,128)(2,1)}), bf16[14,4,32,256]{3,2,0,1:T(8,128)(2,1)S(1)}, u32[]{:S(2)}, u32[]{:S(2)}) async-start(bf16[14,4,32,256]{3,2,0,1:T(8,128)(2,1)} %copy.42), calls=%async_computation.1 | async-start | bytes 1835008 | tf_op jit(solution)/shard_map/all_to_all | solution.py:147
  168.8 1.5 compare_reduce_fusion
  170.3 9.2 %all-to-all-done.1 = bf16[14,4,32,256]{3,2,0,1:T(8,128)(2,1)S(1)} async-done(((bf16[14,4,32,256]{3,2,0,1:T(8,128)(2,1)}), bf16[14,4,32,256]{3,2,0,1:T(8,128)(2,1)S(1)}, u32[]{:S(2)}, u32[]{:S(2)}) %all-to-all-start.1) | async-done | bytes 917536 | tf_op jit(solution)/shard_map/all_to_all | solution.py:147
  179.5 14.9 %all-gather.11.cloned.1.call-done = bf16[1024,9216]{1,0:T(8,128)(2,1)} async-done(((bf16[32,9216]{1,0:T(8,128)(2,1)}), bf16[1024,9216]{1,0:T(8,128)(2,1)}) %all-gather.11.cloned.1.call-update) | async-done | bytes 18874384 | tf_op jit(solution)/shard_map/all_gather | solution.py:129
  194.4 1.5 convolution_convert_fusion.4
  195.9 1.5 convolution_convert_fusion.5
  197.4 1.5 convolution_convert_fusion.6
  198.9 2.2 fusion.33
  201.4 21.6 %fusion.3 = bf16[14,32,4096]{2,1,0:T(8,128)(2,1)S(1)} fusion(bf16[1024,9216]{1,0:T(8,128)(2,1)} %all-gather.11.cloned.1.call-done, f32[14,32,1024]{2,1,0:T(8,128)S(1)} %get-tuple-element.63, f32[1024]{0:T(1024)S(1)} %copy-done.11, f32[1024]{0:T(1024)S(1)} %copy-done.12, f32[14,32]{1,0:T(8,128)S(1)} %add_rsqrt_fusion.1, ...), kind=kOutput, calls=%fused_computation.10 | convolution fusion | flops 3879665664 | bytes 13905408 | tf_op jit(solution)/shard_map/pid,du->piu/dot_general | solution.py:170
  223.0 2.7 fusion.17
  225.8 2.7 fusion.16
  228.5 2.7 fusion.15
  231.3 3.3 %fusion.34 = (f32[14,32]{1,0:T(8,128)S(1)}, f32[14,32,1024]{2,1,0:T(8,128)S(1)}) fusion(bf16[1024,9216]{1,0:T(8,128)(2,1)} %all-gather.11.cloned.1.call-done, bf16[14,32,4096]{2,1,0:T(8,128)(2,1)S(1)} %fusion.3, bf16[14,32,1024]{2,1,0:T(8,128)(2,1)S(1)} %fusion.17, bf16[14,32,1024]{2,1,0:T(8,128)(2,1)S(1)} %fusion.16, ...), kind=kOutput, calls=%fused_computation.106 | convolution fusion | flops 946863680 | bytes 9463552 | tf_op jit(solution)/shard_map/piu,ou->pio/dot_general | solution.py:175
  235.4 0.7 gather_fusion.2
  236.1 1.5 broadcast_select_fusion
  237.6 5.5 %all-to-all-start.2 = ((bf16[32,32,1024]{2,1,0:T(8,128)(2,1)}), bf16[32,32,1024]{2,1,0:T(8,128)(2,1)S(1)}, u32[]{:S(2)}, u32[]{:S(2)}) async-start(bf16[32,32,1024]{2,1,0:T(8,128)(2,1)} %broadcast_select_fusion), calls=%async_computation.2 | async-start | bytes 4194304 | tf_op jit(solution)/shard_map/all_to_all | solution.py:192
  243.2 28.5 %all-to-all-done.2 = bf16[32,32,1024]{2,1,0:T(8,128)(2,1)S(1)} async-done(((bf16[32,32,1024]{2,1,0:T(8,128)(2,1)}), bf16[32,32,1024]{2,1,0:T(8,128)(2,1)S(1)}, u32[]{:S(2)}, u32[]{:S(2)}) %all-to-all-start.2) | async-done | bytes 2097184 | tf_op jit(solution)/shard_map/all_to_all | solution.py:192
  271.7 1.5 gather_fusion.3
  273.3 1.3 pad_maximum_fusion
  274.7 3.6 %copy.43 = bf16[1792,2,256]{2,1,0:T(2,128)(2,1)} copy(bf16[1792,2,256]{0,2,1:T(8,128)(2,1)S(1)} %pad_maximum_fusion) | data formatting | bytes 3670016
  278.2 37.2 %all-gather.13.cloned.1.call-done = bf16[14,128,1024]{2,1,0:T(8,128)(2,1)} async-done(((bf16[14,32,1024]{2,1,0:T(8,128)(2,1)}), bf16[14,128,1024]{2,1,0:T(8,128)(2,1)}) %all-gather.13.cloned.1.call-update) | async-done | bytes 3670032 | tf_op jit(solution)/shard_map/all_gather | solution.py:194
  315.4 4.2 %copy.56 = bf16[1792,1024]{1,0:T(8,128)(2,1)} copy(bf16[1792,1024]{1,0:T(8,128)(2,1)} %bitcast.110) | data formatting | bytes 7340032
  (65 shorter events, 4.2 us)
Async XLA Ops:
  7.2 8.6 %copy-start.4 = (bf16[129,256]{1,0:T(8,128)(2,1)S(1)}, bf16[129,256]{1,0:T(8,128)(2,1)}, u32[]{:S(2)}) copy-start(bf16[129,256]{1,0:T(8,128)(2,1)} %constant.154.clone.1) | copy-start | bytes 198148
  7.2 58.2 %all-gather.7.cloned.1.call-start = ((), (), s32[]{:S(2)}) async-start(), calls=%async_computation.3 | async-start | bytes 1622016 | tf_op jit(solution)/shard_map/all_gather | solution.py:85
  8.6 103.3 %all-gather.9.cloned.1.call-start = ((), (), s32[]{:S(2)}) async-start(), calls=%async_computation.4 | async-start | bytes 4587520 | tf_op jit(solution)/shard_map/all_gather | solution.py:126
  15.7 1.6 copy-start.5
  15.7 1.6 copy-start.6
  15.7 1.6 copy-start.8
  58.2 1.4 copy-start
  65.4 129.1 %all-gather.11.cloned.1.call-start = ((), (), s32[]{:S(2)}) async-start(), calls=%async_computation.5 | async-start | bytes 19464192 | tf_op jit(solution)/shard_map/all_gather | solution.py:129
  113.3 4.6 %copy-start.7 = (s32[1,1,14,128]{3,1,2,0:T(1,128)}, s32[1,1,14,128]{3,1,2,0:T(1,128)S(1)}, u32[]{:S(2)}) copy-start(s32[1,1,14,128]{3,1,2,0:T(1,128)S(1)} %copy.52) | copy-start | bytes 21508
  122.9 5.2 %copy-start.1 = (bf16[1792,256]{0,1:T(8,128)(2,1)}, bf16[1792,256]{0,1:T(8,128)(2,1)S(1)}, u32[]{:S(2)}) copy-start(bf16[1792,256]{0,1:T(8,128)(2,1)S(1)} %convolution_convert_fusion.1) | copy-start | bytes 2752516
  128.1 34.7 %copy-start.3 = (bf16[1792,256]{0,1:T(8,128)(2,1)}, bf16[1792,256]{0,1:T(8,128)(2,1)S(1)}, u32[]{:S(2)}) copy-start(bf16[1792,256]{0,1:T(8,128)(2,1)S(1)} %convolution_convert_fusion) | copy-start | bytes 2752516
  164.9 14.6 %all-to-all-start.1 = ((bf16[14,4,32,256]{3,2,0,1:T(8,128)(2,1)}), bf16[14,4,32,256]{3,2,0,1:T(8,128)(2,1)S(1)}, u32[]{:S(2)}, u32[]{:S(2)}) async-start(bf16[14,4,32,256]{3,2,0,1:T(8,128)(2,1)} %copy.42), calls=%async_computation.1 | async-start | bytes 1835008 | tf_op jit(solution)/shard_map/all_to_all | solution.py:147
  198.9 2.5 copy-start.11
  198.9 2.5 copy-start.12
  231.3 3.7 %copy-start.9 = (f32[1024]{0:T(1024)S(1)}, f32[1024]{0:T(1024)}, u32[]{:S(2)}) copy-start(f32[1024]{0:T(1024)} %param.31) | copy-start | bytes 12292
  231.3 3.7 %copy-start.10 = (f32[1024]{0:T(1024)S(1)}, f32[1024]{0:T(1024)}, u32[]{:S(2)}) copy-start(f32[1024]{0:T(1024)} %param.30) | copy-start | bytes 12292
  237.6 35.7 %copy-start.2 = (bf16[1792,256]{0,1:T(8,128)(2,1)S(1)}, bf16[1792,256]{0,1:T(8,128)(2,1)}, u32[]{:S(2)}) copy-start(bf16[1792,256]{0,1:T(8,128)(2,1)} %copy-done.1) | copy-start | bytes 2752516
  237.6 34.1 %all-to-all-start.2 = ((bf16[32,32,1024]{2,1,0:T(8,128)(2,1)}), bf16[32,32,1024]{2,1,0:T(8,128)(2,1)S(1)}, u32[]{:S(2)}, u32[]{:S(2)}) async-start(bf16[32,32,1024]{2,1,0:T(8,128)(2,1)} %broadcast_select_fusion), calls=%async_computation.2 | async-start | bytes 4194304 | tf_op jit(solution)/shard_map/all_to_all | solution.py:192
  243.1 72.3 %all-gather.13.cloned.1.call-start = ((), (), s32[]{:S(2)}) async-start(), calls=%async_computation.6 | async-start | bytes 4587520 | tf_op jit(solution)/shard_map/all_gather | solution.py:194
Sparse Core Ops, SparseCore 0:
  10.2 55.0 all-gather.6
  67.6 44.2 all-gather.8
  114.1 80.2 all-gather.10
  273.4 41.9 all-gather.12

commit v3 on v2

--- a/solution.py
+++ b/solution.py
@@ -166,32 +166,43 @@
     first_mine = layer_norm(
         dealt_mine.astype(jnp.float32) + attended, gain_first, shift_first
     ).astype(jnp.bfloat16)
-    hidden = jax.nn.gelu(
-        jnp.einsum("pid,du->piu", first_mine, full_up, preferred_element_type=jnp.float32),
-        approximate=False,
-    ).astype(jnp.bfloat16)
-    fed = jnp.zeros((pages_dev, sub, width), jnp.float32)
-    for group in range(n_model):
-        term = jnp.einsum(
-            "piu,ou->pio",
-            hidden[:, :, group * unit_part : (group + 1) * unit_part],
-            down_t[:, group * unit_part : (group + 1) * unit_part],
-            preferred_element_type=jnp.float32,
+    def feed_forward(first_rows):
+        hidden = jax.nn.gelu(
+            jnp.einsum("pid,du->piu", first_rows, full_up, preferred_element_type=jnp.float32),
+            approximate=False,
         ).astype(jnp.bfloat16)
-        fed = fed + term.astype(jnp.float32)
-    second_mine = layer_norm(first_mine.astype(jnp.float32) + fed, gain_second, shift_second).astype(
-        jnp.bfloat16
-    )
+        fed = jnp.zeros(first_rows.shape, jnp.float32)
+        for group in range(n_model):
+            term = jnp.einsum(
+                "piu,ou->pio",
+                hidden[:, :, group * unit_part : (group + 1) * unit_part],
+                down_t[:, group * unit_part : (group + 1) * unit_part],
+                preferred_element_type=jnp.float32,
+            ).astype(jnp.bfloat16)
+            fed = fed + term.astype(jnp.float32)
+        return layer_norm(
+            first_rows.astype(jnp.float32) + fed, gain_second, shift_second
+        ).astype(jnp.bfloat16)
 
     valid = got_slots >= 0
-    outgoing = jnp.where(
-        valid[:, None, None],
-        second_mine[jnp.clip(got_slots, 0, pages_dev - 1)],
-        jnp.zeros((), second_mine.dtype),
-    )
-    returned = lax.all_to_all(outgoing, "dp", split_axis=0, concat_axis=0, tiled=True)
-    mixed_mine = returned[position]
-    mixed = lax.all_gather(mixed_mine, "mp", axis=1).reshape(pages_dev * page, width)
+    piece = sub // 2
+    pieces = []
+    rest = first_mine[:, piece:]
+    for at in (0, piece):
+        if at == 0:
+            second_rows = feed_forward(first_mine[:, :piece])
+        else:
+            rest, outgoing = lax.optimization_barrier((rest, outgoing))
+            second_rows = feed_forward(rest)
+        outgoing = jnp.where(
+            valid[:, None, None],
+            second_rows[jnp.clip(got_slots, 0, pages_dev - 1)],
+            jnp.zeros((), second_rows.dtype),
+        )
+        returned = lax.all_to_all(outgoing, "dp", split_axis=0, concat_axis=0, tiled=True)
+        pieces.append(returned[position])
+    pieces = [lax.all_gather(part, "mp", axis=1) for part in pieces]
+    mixed = jnp.concatenate(pieces, axis=2).reshape(pages_dev * page, width)
     kv_cache = jnp.stack([keys, values], axis=1)
     return (mixed, kv_cache)
 

time: 327 us -> 324 us (level)
  waiting for transfers between devices: 126 us -> 83.3 us
  blocking collectives: 52.4 us -> 76.6 us
  matrix products: 49.9 us -> 62 us
  other arithmetic: 14.2 us -> 19.1 us
    all_to_all x1, waiting for transfers between devices: 28.5 us -> 0.01 us  [body(): lax.all_to_all(outgoing, 'dp', split_axis=0, concat_axis=0, tiled=True)]
    all_to_all x0 -> x1, blocking collectives: none -> 24.2 us  [body(): lax.all_to_all(outgoing, 'dp', split_axis=0, concat_axis=0, tiled=True)]
    all_gather x1 -> x2, waiting for transfers between devices: 37.2 us -> 23 us  [body(): pieces = [lax.all_gather(part, 'mp', axis=1) for part in pieces]]
    dot_general x5 -> x10, matrix products: 33.1 us -> 45.3 us  [the longest x2 23.8 us: feed_forward(): jnp.einsum('pid,du->piu', first_rows, full_up, preferred_element_type=jnp...]
    concatenate x0 -> x1, other arithmetic: none -> 4.57 us  [body(): mixed = jnp.concatenate(pieces, axis=2).reshape(pages_dev * page, width)]
    unnamed x33 -> x32, local copies, waits for them, and re-layouts: 10.4 us -> 6.19 us
  transfers between devices with their start and end apart: 6 -> 7, of which waited for: 6 -> 5; matrix products, arithmetic and copies ran while one was open for 12% -> 20% of each run, Pallas kernels for 10% -> 10%
where the time goes in v3:
time: 324 us; the launch traced here: 323 us
  waiting for transfers between devices  83.3 us (26%)
  blocking collectives  76.6 us (24%)
  matrix products  62 us (19%)
  Pallas kernels  32.9 us (10%)
  local copies, waits for them, and re-layouts  24.6 us (8%)
  other arithmetic  19.1 us (6%)
  between operations  14.4 us (4%)
  starting transfers between devices  9.69 us (3%)
    all_to_all x1, blocking collectives, body(): lax.all_to_all(send_pages, 'dp', split_axis=0, concat_axis=0, tiled=True)  40.9 us
    all_gather x1, waiting for transfers between devices, body(): lax.all_gather(dealt_part, 'mp', axis=2, tiled=True)  33.2 us
    pallas_call x1, Pallas kernels, attention(): pl.pallas_call(_attn_kernel, out_shape=jax.ShapeDtypeStruct((rows, heads...  32.9 us
    all_to_all x1, blocking collectives, body(): lax.all_to_all(outgoing, 'dp', split_axis=0, concat_axis=0, tiled=True)  24.2 us
    dot_general x2, matrix products, feed_forward(): jnp.einsum('pid,du->piu', first_rows, full_up, preferred_element_type=jnp...  23.8 us
    all_gather x2, waiting for transfers between devices, body(): pieces = [lax.all_gather(part, 'mp', axis=1) for part in pieces]  23 us
    dot_general x8, matrix products, feed_forward(): jnp.einsum('piu,ou->pio', hidden[:, :, group * unit_part:(group + 1) * un...  21.5 us
    all_gather x1, waiting for transfers between devices, body(): ffn_gathered = lax.all_gather(ffn_local, 'dp', axis=0, tiled=True)  14.9 us
  transfers between devices with their start and end apart: 7, of which 5 were waited for; matrix products, arithmetic and copies ran while one was open for 20% of the time, Pallas kernels for 10%

profile of v3, /device:TPU:1, one launch (start us, length us, event | category | flops | bytes accessed | tf_op | source)
XLA Modules:
  0.0 322.6 jit_solution(8573828663807207424)
XLA Ops:
  7.2 1.4 pad_maximum_fusion.5
  10.9 1.4 and_reduce_fusion
  12.3 1.4 broadcast_select_fusion.2
  14.4 1.2 constant_dynamic-slice_fusion
  15.9 1.3 scatter_fusion
  17.3 40.9 %all_to_all.20 = bf16[32,129,256]{2,1,0:T(8,128)(2,1)S(1)} all-to-all(bf16[32,129,256]{2,1,0:T(8,128)(2,1)S(1)} %scatter_fusion), channel_id=1, replica_groups=mesh['dp'=32,'mp'=4] {'dp'}, dimensions={0} | all-to-all | bytes 4227072 | tf_op jit(solution)/shard_map/all_to_all | solution.py:110
  58.5 1.1 copy-done
  59.6 1.2 clamp_reduce_fusion
  60.9 1.5 gather_fusion
  62.5 2.9 all-gather.9.cloned.1.call-done
  65.4 11.5 %all-gather = bf16[32,9216]{1,0:T(8,128)(2,1)S(1)} all-gather(bf16[32,2304]{1,0:T(8,128)(2,1)S(1)} %pad_maximum_fusion.4), channel_id=2, replica_groups=mesh['dp'=32,'mp'=4] {'mp'}, dimensions={1}, use_global_device_ids=true | all-gather | bytes 737280 | tf_op jit(solution)/shard_map/all_gather | solution.py:118
  78.6 33.2 %all-gather.11.cloned.1.call-done = bf16[14,128,1024]{2,1,0:T(8,128)(2,1)} async-done(((bf16[14,128,256]{2,1,0:T(8,128)(2,1)}), bf16[14,128,1024]{2,1,0:T(8,128)(2,1)}) %all-gather.11.cloned.1.call-update) | async-done | bytes 3670032 | tf_op jit(solution)/shard_map/all_gather | solution.py:126
  113.4 1.3 copy.49
  114.6 3.3 %convolution_convert_fusion.2 = bf16[1792,256]{0,1:T(8,128)(2,1)S(1)} fusion(bf16[1792,1024]{1,0:T(8,128)(2,1)} %bitcast.181, bf16[1024,768]{1,0:T(8,128)(2,1)} %all-gather.9.cloned.1.call-done), kind=kOutput, calls=%fused_computation.51 | convolution fusion | flops 939982848 | bytes 5111808 | tf_op jit(solution)/shard_map/dot_general | solution.py:136
  118.0 1.6 copy.38
  119.6 3.3 %convolution_convert_fusion.1 = bf16[1792,256]{0,1:T(8,128)(2,1)S(1)} fusion(bf16[1792,1024]{1,0:T(8,128)(2,1)} %bitcast.182, bf16[1024,768]{1,0:T(8,128)(2,1)} %all-gather.9.cloned.1.call-done), kind=kOutput, calls=%fused_computation.50 | convolution fusion | flops 939982848 | bytes 5111808 | tf_op jit(solution)/shard_map/dot_general | solution.py:137
  122.9 1.7 copy.39
  124.6 3.5 %convolution_convert_fusion = bf16[1792,256]{0,1:T(8,128)(2,1)S(1)} fusion(bf16[1792,1024]{1,0:T(8,128)(2,1)} %bitcast.183, bf16[1024,768]{1,0:T(8,128)(2,1)} %all-gather.9.cloned.1.call-done), kind=kOutput, calls=%fused_computation.49 | convolution fusion | flops 939982848 | bytes 5111808 | tf_op jit(solution)/shard_map/dot_general | solution.py:138
  128.1 1.7 copy.40
  129.8 32.9 %shard_map.140 = bf16[1792,256]{1,0:T(8,128)(2,1)} custom-call(bf16[4,1792,64]{2,1,0:T(8,128)(2,1)} %bitcast.168, bf16[4,1792,64]{2,1,0:T(8,128)(2,1)} %bitcast.169, bf16[4,1792,64]{2,1,0:T(8,128)(2,1)} %bitcast.170, s32[1792,1]{1,0:T(8,128)} %bitcast.176, s32[1,1792]{1,0:T(1,128)} %bitcast.188), custom_call_target="tpu_custom_call" | custom-call | flops 3288334336 | bytes 3670016 | tf_op jit(solution)/shard_map/pallas_call | solution.py:35
  162.7 2.2 copy.42
  164.9 3.8 %all-to-all-start.1 = ((bf16[14,4,32,256]{3,2,0,1:T(8,128)(2,1)}), bf16[14,4,32,256]{3,2,0,1:T(8,128)(2,1)S(1)}, u32[]{:S(2)}, u32[]{:S(2)}) async-start(bf16[14,4,32,256]{3,2,0,1:T(8,128)(2,1)} %copy.42), calls=%async_computation.1 | async-start | bytes 1835008 | tf_op jit(solution)/shard_map/all_to_all | solution.py:147
  168.8 1.5 compare_reduce_fusion
  170.3 9.2 %all-to-all-done.1 = bf16[14,4,32,256]{3,2,0,1:T(8,128)(2,1)S(1)} async-done(((bf16[14,4,32,256]{3,2,0,1:T(8,128)(2,1)}), bf16[14,4,32,256]{3,2,0,1:T(8,128)(2,1)S(1)}, u32[]{:S(2)}, u32[]{:S(2)}) %all-to-all-start.1) | async-done | bytes 917536 | tf_op jit(solution)/shard_map/all_to_all | solution.py:147
  179.5 14.9 %all-gather.13.cloned.1.call-done = bf16[1024,9216]{1,0:T(8,128)(2,1)} async-done(((bf16[32,9216]{1,0:T(8,128)(2,1)}), bf16[1024,9216]{1,0:T(8,128)(2,1)}) %all-gather.13.cloned.1.call-update) | async-done | bytes 18874384 | tf_op jit(solution)/shard_map/all_gather | solution.py:129
  194.4 1.5 convolution_convert_fusion.4
  195.9 1.5 convolution_convert_fusion.5
  197.4 1.5 convolution_convert_fusion.6
  198.9 2.2 fusion.75
  201.9 11.9 %fusion.4 = bf16[14,16,4096]{2,1,0:T(8,128)(2,1)S(1)} fusion(bf16[1024,9216]{1,0:T(8,128)(2,1)} %all-gather.13.cloned.1.call-done, bf16[14,32,1024]{2,1,0:T(8,128)(2,1)S(1)} %add_convert_fusion), kind=kOutput, calls=%fused_computation.14 | convolution fusion | flops 1938685952 | bytes 10682368 | tf_op jit(solution)/shard_map/pid,du->piu/dot_general | solution.py:171
  213.8 2.4 fusion.53
  216.2 2.4 fusion.51
  218.6 2.4 fusion.49
  221.0 2.6 fusion.76
  224.7 1.1 broadcast_select_fusion.1
  225.8 5.4 %all-to-all-start.2 = ((bf16[32,16,1024]{2,1,0:T(8,128)(2,1)}), bf16[32,16,1024]{2,1,0:T(8,128)(2,1)S(1)}, u32[]{:S(2)}, u32[]{:S(2)}) async-start(bf16[32,16,1024]{2,1,0:T(8,128)(2,1)} %broadcast_select_fusion.1), calls=%async_computation.2 | async-start | bytes 2097152 | tf_op jit(solution)/shard_map/all_to_all | solution.py:202
  231.5 11.9 %fusion.7 = bf16[14,16,4096]{2,1,0:T(8,128)(2,1)S(1)} fusion(bf16[14,16,1024]{2,1,0:T(8,128)(2,1)S(1)} %slice.247, bf16[1024,9216]{1,0:T(8,128)(2,1)} %all-gather.13.cloned.1.call-done), kind=kOutput, calls=%fused_computation.17 | convolution fusion | flops 1938685952 | bytes 10682368 | tf_op jit(solution)/shard_map/pid,du->piu/dot_general | solution.py:171
  243.5 3.0 fusion.52
  246.5 3.3 %fusion.50 = f32[14,16,1024]{2,1,0:T(8,128)} fusion(bf16[1024,9216]{1,0:T(8,128)(2,1)} %all-gather.13.cloned.1.call-done, bf16[14,16,4096]{2,1,0:T(8,128)(2,1)S(1)} %fusion.7), kind=kOutput, calls=%fused_computation.92 | convolution fusion | flops 470220800 | bytes 3473408 | tf_op jit(solution)/shard_map/piu,ou->pio/dot_general | solution.py:176
  249.9 1.4 gather_fusion.3
  251.3 2.6 fusion.48
  253.9 2.8 fusion.77
  258.0 24.2 %all_to_all.21 = bf16[32,16,1024]{2,1,0:T(8,128)(2,1)S(1)} all-to-all(bf16[32,16,1024]{2,1,0:T(8,128)(2,1)S(1)} %broadcast_select_fusion), channel_id=1, replica_groups=mesh['dp'=32,'mp'=4] {'dp'}, dimensions={0} | all-to-all | bytes 2097152 | tf_op jit(solution)/shard_map/all_to_all | solution.py:202
  282.2 1.3 gather_fusion.5
  283.6 1.3 pad_maximum_fusion.1
  284.9 3.6 %copy.43 = bf16[1792,2,256]{2,1,0:T(2,128)(2,1)} copy(bf16[1792,2,256]{0,2,1:T(8,128)(2,1)S(1)} %pad_maximum_fusion.1) | data formatting | bytes 3670016
  288.5 23.0 %all-gather.17.cloned.1.call-done = bf16[14,64,1024]{2,1,0:T(8,128)(2,1)} async-done(((bf16[14,16,1024]{2,1,0:T(8,128)(2,1)}), bf16[14,64,1024]{2,1,0:T(8,128)(2,1)}) %all-gather.17.cloned.1.call-update) | async-done | bytes 1835024 | tf_op jit(solution)/shard_map/all_gather | solution.py:204
  311.5 4.6 %pad_maximum_fusion = bf16[14,4,32,1024]{3,2,1,0:T(8,128)(2,1)} fusion(bf16[14,4,16,1024]{3,2,1,0:T(8,128)(2,1)} %bitcast.167, bf16[14,4,16,1024]{3,2,1,0:T(8,128)(2,1)} %bitcast.166), kind=kLoop, calls=%fused_computation.18 | loop fusion | flops 7340032 | bytes 7340032 | tf_op jit(solution)/shard_map/concatenate | solution.py:205
  (83 shorter events, 10.4 us)
Async XLA Ops:
  7.2 8.6 %copy-start.4 = (bf16[129,256]{1,0:T(8,128)(2,1)S(1)}, bf16[129,256]{1,0:T(8,128)(2,1)}, u32[]{:S(2)}) copy-start(bf16[129,256]{1,0:T(8,128)(2,1)} %constant.158.clone.1) | copy-start | bytes 198148
  7.2 58.2 %all-gather.9.cloned.1.call-start = ((), (), s32[]{:S(2)}) async-start(), calls=%async_computation.4 | async-start | bytes 1622016 | tf_op jit(solution)/shard_map/all_gather | solution.py:85
  8.6 103.3 %all-gather.11.cloned.1.call-start = ((), (), s32[]{:S(2)}) async-start(), calls=%async_computation.5 | async-start | bytes 4587520 | tf_op jit(solution)/shard_map/all_gather | solution.py:126
  15.7 1.6 copy-start.5
  15.7 1.6 copy-start.6
  15.7 1.6 copy-start.10
  58.2 1.4 copy-start
  65.4 129.1 %all-gather.13.cloned.1.call-start = ((), (), s32[]{:S(2)}) async-start(), calls=%async_computation.6 | async-start | bytes 19464192 | tf_op jit(solution)/shard_map/all_gather | solution.py:129
  113.4 4.6 %copy-start.7 = (s32[1,1,14,128]{3,1,2,0:T(1,128)}, s32[1,1,14,128]{3,1,2,0:T(1,128)S(1)}, u32[]{:S(2)}) copy-start(s32[1,1,14,128]{3,1,2,0:T(1,128)S(1)} %copy.52) | copy-start | bytes 21508
  128.1 34.6 %copy-start.1 = (bf16[1792,256]{0,1:T(8,128)(2,1)}, bf16[1792,256]{0,1:T(8,128)(2,1)S(1)}, u32[]{:S(2)}) copy-start(bf16[1792,256]{0,1:T(8,128)(2,1)S(1)} %convolution_convert_fusion) | copy-start | bytes 2752516
  164.9 14.6 %all-to-all-start.1 = ((bf16[14,4,32,256]{3,2,0,1:T(8,128)(2,1)}), bf16[14,4,32,256]{3,2,0,1:T(8,128)(2,1)S(1)}, u32[]{:S(2)}, u32[]{:S(2)}) async-start(bf16[14,4,32,256]{3,2,0,1:T(8,128)(2,1)} %copy.42), calls=%async_computation.1 | async-start | bytes 1835008 | tf_op jit(solution)/shard_map/all_to_all | solution.py:147
  198.9 2.5 copy-start.11
  198.9 2.5 copy-start.12
  220.9 2.9 copy-start.8
  221.0 2.9 copy-start.9
  225.8 24.0 %all-to-all-start.2 = ((bf16[32,16,1024]{2,1,0:T(8,128)(2,1)}), bf16[32,16,1024]{2,1,0:T(8,128)(2,1)S(1)}, u32[]{:S(2)}, u32[]{:S(2)}) async-start(bf16[32,16,1024]{2,1,0:T(8,128)(2,1)} %broadcast_select_fusion.1), calls=%async_computation.2 | async-start | bytes 2097152 | tf_op jit(solution)/shard_map/all_to_all | solution.py:202
  231.2 57.3 %all-gather.15.cloned.1.call-start = ((), (), s32[]{:S(2)}) async-start(), calls=%async_computation.7 | async-start | bytes 2293760 | tf_op jit(solution)/shard_map/all_gather | solution.py:204
  243.4 3.1 copy-start.3
  251.3 2.7 copy-start.2
  251.3 60.2 %all-gather.17.cloned.1.call-start = ((), (), s32[]{:S(2)}) async-start(), calls=%async_computation.8 | async-start | bytes 2293760 | tf_op jit(solution)/shard_map/all_gather | solution.py:204
Sparse Core Ops, SparseCore 0:
  10.2 55.0 all-gather.8
  67.6 44.2 all-gather.10
  114.1 80.2 all-gather.12
  251.4 29.3 all-gather.14
  283.7 27.7 all-gather.16

commit v4 on v3

--- a/solution.py
+++ b/solution.py
@@ -83,9 +83,6 @@
     unit_part = w_up.shape[1]
     attn_local = jnp.concatenate([w_query, w_key, w_value], axis=1)
     attn_gathered = lax.all_gather(attn_local, "dp", axis=0, tiled=True)
-    full_query = attn_gathered[:, :head_cols]
-    full_key = attn_gathered[:, head_cols : 2 * head_cols]
-    full_value = attn_gathered[:, 2 * head_cols : 3 * head_cols]
     small = jnp.concatenate([w_out.T, w_up, w_down.T], axis=1)
 
     target = page_table // pages_dev
@@ -133,16 +130,20 @@
     full_up = ffn_gathered[:, in_all : in_all + units]
     down_t = ffn_gathered[:, in_all + units :]
 
-    query = jnp.dot(dealt, full_query, preferred_element_type=jnp.float32).astype(jnp.bfloat16)
-    keys = jnp.dot(dealt, full_key, preferred_element_type=jnp.float32).astype(jnp.bfloat16)
-    values = jnp.dot(dealt, full_value, preferred_element_type=jnp.float32).astype(jnp.bfloat16)
-    heads_here = query.shape[1] // HEAD
-    rows = query.shape[0]
-
-    def by_head(x):
-        return x.reshape(rows, heads_here, HEAD).transpose(1, 0, 2)
-
-    context = attention(by_head(query), by_head(keys), by_head(values), dealt_ids)
+    projected = jnp.dot(dealt, attn_gathered, preferred_element_type=jnp.float32).astype(
+        jnp.bfloat16
+    )
+    keys = projected[:, head_cols : 2 * head_cols]
+    values = projected[:, 2 * head_cols :]
+    heads_here = head_cols // HEAD
+    rows = projected.shape[0]
+    by_head = projected.reshape(rows, 3 * heads_here, HEAD).transpose(1, 0, 2)
+    context = attention(
+        by_head[:heads_here],
+        by_head[heads_here : 2 * heads_here],
+        by_head[2 * heads_here :],
+        dealt_ids,
+    )
 
     context_rows = lax.all_to_all(
         context.reshape(pages_dev, n_model, sub, head_cols),

time: 324 us -> 349 us (1.077)
  waiting for transfers between devices: 83.3 us -> 104 us
  local copies, waits for them, and re-layouts: 24.6 us -> 34.5 us
  matrix products: 62 us -> 56.1 us
    all_to_all x1, waiting for transfers between devices: 0.01 us -> 17 us  [body(): lax.all_to_all(outgoing, 'dp', split_axis=0, concat_axis=0, tiled=True)]
    slice x0 -> x1, local copies, waits for them, and re-layouts: none -> 5.49 us  [body(): by_head[2 * heads_here:]]
    all_gather x2, waiting for transfers between devices: 23 us -> 28.3 us  [body(): pieces = [lax.all_gather(part, 'mp', axis=1) for part in pieces]]
    dot_general x3 -> x1, matrix products: 10.1 us -> 5.58 us  [body(): jnp.dot(dealt, attn_gathered, preferred_element_type=jnp.float32)]
  transfers between devices with their start and end apart: 7 -> 7, of which waited for: 5 -> 6; matrix products, arithmetic and copies ran while one was open for 20% -> 12% of each run, Pallas kernels for 10% -> 9%
where the time goes in v4:
time: 349 us; the launch traced here: 348 us
  waiting for transfers between devices  104 us (30%)
  blocking collectives  74.3 us (21%)
  matrix products  56.1 us (16%)
  local copies, waits for them, and re-layouts  34.5 us (10%)
  Pallas kernels  32.9 us (9%)
  other arithmetic  21.4 us (6%)
  between operations  14.3 us (4%)
  starting transfers between devices  10.1 us (3%)
    all_to_all x1, blocking collectives, body(): lax.all_to_all(send_pages, 'dp', split_axis=0, concat_axis=0, tiled=True)  40.9 us
    all_gather x1, waiting for transfers between devices, body(): lax.all_gather(dealt_part, 'mp', axis=2, tiled=True)  33.2 us
    pallas_call x1, Pallas kernels, attention(): pl.pallas_call(_attn_kernel, out_shape=jax.ShapeDtypeStruct((rows, heads...  32.9 us
    all_gather x2, waiting for transfers between devices, body(): pieces = [lax.all_gather(part, 'mp', axis=1) for part in pieces]  28.3 us
    dot_general x2, matrix products, feed_forward(): jnp.einsum('pid,du->piu', first_rows, full_up, preferred_element_type=jnp...  23.9 us
    all_to_all x1, blocking collectives, body(): lax.all_to_all(outgoing, 'dp', split_axis=0, concat_axis=0, tiled=True)  21.9 us
    dot_general x8, matrix products, feed_forward(): jnp.einsum('piu,ou->pio', hidden[:, :, group * unit_part:(group + 1) * un...  19.5 us
    all_to_all x1, waiting for transfers between devices, body(): lax.all_to_all(outgoing, 'dp', split_axis=0, concat_axis=0, tiled=True)  17 us
  transfers between devices with their start and end apart: 7, of which 6 were waited for; matrix products, arithmetic and copies ran while one was open for 12% of the time, Pallas kernels for 9%

profile of v4, /device:TPU:1, one launch (start us, length us, event | category | flops | bytes accessed | tf_op | source)
XLA Modules:
  0.0 347.7 jit_solution(11509643295912311001)
XLA Ops:
  7.2 1.4 pad_maximum_fusion.5
  10.9 1.2 constant_dynamic-slice_fusion
  12.2 1.4 and_reduce_fusion
  13.6 1.4 broadcast_select_fusion.2
  16.0 1.3 scatter_fusion
  17.4 40.9 %all_to_all.20 = bf16[32,129,256]{2,1,0:T(8,128)(2,1)S(1)} all-to-all(bf16[32,129,256]{2,1,0:T(8,128)(2,1)S(1)} %scatter_fusion), channel_id=1, replica_groups=mesh['dp'=32,'mp'=4] {'dp'}, dimensions={0} | all-to-all | bytes 4227072 | tf_op jit(solution)/shard_map/all_to_all | solution.py:107
  58.5 1.1 copy-done
  59.6 1.2 clamp_reduce_fusion
  61.0 1.5 gather_fusion
  62.5 1.9 all-gather.9.cloned.1.call-done
  64.5 11.6 %all-gather = bf16[32,9216]{1,0:T(8,128)(2,1)S(1)} all-gather(bf16[32,2304]{1,0:T(8,128)(2,1)S(1)} %pad_maximum_fusion.4), channel_id=2, replica_groups=mesh['dp'=32,'mp'=4] {'mp'}, dimensions={1}, use_global_device_ids=true | all-gather | bytes 737280 | tf_op jit(solution)/shard_map/all_gather | solution.py:115
  77.9 33.2 %all-gather.11.cloned.1.call-done = bf16[14,128,1024]{2,1,0:T(8,128)(2,1)} async-done(((bf16[14,128,256]{2,1,0:T(8,128)(2,1)}), bf16[14,128,1024]{2,1,0:T(8,128)(2,1)}) %all-gather.11.cloned.1.call-update) | async-done | bytes 3670032 | tf_op jit(solution)/shard_map/all_gather | solution.py:123
  112.6 1.3 copy.43
  113.9 5.6 %convolution_convert_fusion = bf16[1792,768]{0,1:T(8,128)(2,1)S(1)} fusion(bf16[1792,1024]{1,0:T(8,128)(2,1)} %bitcast.171, bf16[1024,768]{1,0:T(8,128)(2,1)} %all-gather.9.cloned.1.call-done), kind=kOutput, calls=%fused_computation.49 | convolution fusion | flops 2819948544 | bytes 7995392 | tf_op jit(solution)/shard_map/dot_general | solution.py:133
  119.5 4.3 %copy.34 = bf16[1792,12,64]{2,0,1:T(8,128)(2,1)} copy(bf16[1792,12,64]{0,2,1:T(8,128)(2,1)S(1)} %bitcast.157) | data formatting | bytes 5505024 | tf_op jit(solution)/shard_map/reshape | solution.py:140
  123.7 5.5 %fusion.71 = (bf16[4,1792,64]{2,1,0:T(8,128)(2,1)}, bf16[4,1792,64]{2,1,0:T(8,128)(2,1)}, bf16[4,1792,64]{2,1,0:T(8,128)(2,1)}) fusion(bf16[12,1792,64]{2,1,0:T(8,128)(2,1)} %bitcast.156), kind=kLoop, calls=%fused_computation.157 | loop fusion | bytes 5505024 | tf_op jit(solution)/shard_map/slice | solution.py:144
  129.2 32.9 %shard_map.140 = bf16[1792,256]{1,0:T(8,128)(2,1)} custom-call(bf16[4,1792,64]{2,1,0:T(8,128)(2,1)} %get-tuple-element.64.q_ref, bf16[4,1792,64]{2,1,0:T(8,128)(2,1)} %get-tuple-element.63.k_ref, bf16[4,1792,64]{2,1,0:T(8,128)(2,1)} %get-tuple-element.62.v_ref, s32[1792,1]{1,0:T(8,128)} %bitcast.167, s32[1,1792]{1,0:T(1,128)} %bitcast.176), custom_call_target="tpu_custom_call" | custom-call | flops 3288334336 | bytes 3670016 | tf_op jit(solution)/shard_map/pallas_call | solution.py:35
  162.1 2.2 copy.36
  164.3 4.5 %all-to-all-start.1 = ((bf16[14,4,32,256]{3,2,0,1:T(8,128)(2,1)}), bf16[14,4,32,256]{3,2,0,1:T(8,128)(2,1)}, u32[]{:S(2)}, u32[]{:S(2)}) async-start(bf16[14,4,32,256]{3,2,0,1:T(8,128)(2,1)} %copy.36), calls=%async_computation.1 | async-start | bytes 1835008 | tf_op jit(solution)/shard_map/all_to_all | solution.py:148
  168.8 1.5 compare_reduce_fusion
  170.3 9.6 %all-to-all-done.1 = bf16[14,4,32,256]{3,2,0,1:T(8,128)(2,1)} async-done(((bf16[14,4,32,256]{3,2,0,1:T(8,128)(2,1)}), bf16[14,4,32,256]{3,2,0,1:T(8,128)(2,1)}, u32[]{:S(2)}, u32[]{:S(2)}) %all-to-all-start.1) | async-done | bytes 917536 | tf_op jit(solution)/shard_map/all_to_all | solution.py:148
  180.0 13.7 %all-gather.13.cloned.1.call-done = bf16[1024,9216]{1,0:T(8,128)(2,1)} async-done(((bf16[32,9216]{1,0:T(8,128)(2,1)}), bf16[1024,9216]{1,0:T(8,128)(2,1)}) %all-gather.13.cloned.1.call-update) | async-done | bytes 18874384 | tf_op jit(solution)/shard_map/all_gather | solution.py:126
  193.7 1.6 convolution_convert_fusion.4
  195.3 1.6 convolution_convert_fusion.3
  196.9 1.6 convolution_convert_fusion.2
  198.5 2.3 fusion.73
  202.4 11.9 %fusion.4 = bf16[14,16,4096]{2,1,0:T(8,128)(2,1)S(1)} fusion(bf16[1024,9216]{1,0:T(8,128)(2,1)} %all-gather.13.cloned.1.call-done, bf16[14,32,1024]{2,1,0:T(8,128)(2,1)S(1)} %add_convert_fusion), kind=kOutput, calls=%fused_computation.14 | convolution fusion | flops 1938685952 | bytes 10682368 | tf_op jit(solution)/shard_map/pid,du->piu/dot_general | solution.py:172
  214.3 2.4 fusion.49
  216.6 2.4 fusion.51
  219.0 2.4 fusion.53
  221.4 2.6 fusion.74
  224.6 1.6 gather_fusion.2
  226.2 2.3 broadcast_select_fusion.1
  228.5 12.0 %fusion.7 = bf16[14,16,4096]{2,1,0:T(8,128)(2,1)S(1)} fusion(bf16[14,16,1024]{2,1,0:T(8,128)(2,1)} %slice.255, bf16[1024,9216]{1,0:T(8,128)(2,1)} %all-gather.13.cloned.1.call-done), kind=kOutput, calls=%fused_computation.17 | convolution fusion | flops 1938685952 | bytes 10682368 | tf_op jit(solution)/shard_map/pid,du->piu/dot_general | solution.py:172
  240.5 2.4 fusion.48
  242.9 2.4 fusion.50
  245.3 2.4 fusion.52
  247.7 2.6 fusion.75
  250.8 1.6 gather_fusion.4
  252.4 2.3 broadcast_select_fusion
  254.7 5.5 %all-to-all-start.3 = ((bf16[32,16,1024]{2,1,0:T(8,128)(2,1)}), bf16[32,16,1024]{2,1,0:T(8,128)(2,1)}, u32[]{:S(2)}, u32[]{:S(2)}) async-start(bf16[32,16,1024]{2,1,0:T(8,128)(2,1)} %broadcast_select_fusion), calls=%async_computation.3 | async-start | bytes 2097152 | tf_op jit(solution)/shard_map/all_to_all | solution.py:203
  260.3 17.0 %all-to-all-done.3 = bf16[32,16,1024]{2,1,0:T(8,128)(2,1)} async-done(((bf16[32,16,1024]{2,1,0:T(8,128)(2,1)}), bf16[32,16,1024]{2,1,0:T(8,128)(2,1)}, u32[]{:S(2)}, u32[]{:S(2)}) %all-to-all-start.3) | async-done | bytes 1048608 | tf_op jit(solution)/shard_map/all_to_all | solution.py:203
  277.3 2.6 gather_fusion.5
  280.0 21.9 %all_to_all.21 = bf16[32,16,1024]{2,1,0:T(8,128)(2,1)} all-to-all(bf16[32,16,1024]{2,1,0:T(8,128)(2,1)} %broadcast_select_fusion.1), channel_id=1, replica_groups=mesh['dp'=32,'mp'=4] {'dp'}, dimensions={0} | all-to-all | bytes 2097152 | tf_op jit(solution)/shard_map/all_to_all | solution.py:203
  301.8 2.6 gather_fusion.3
  304.7 3.6 %copy.37 = bf16[1792,2,256]{2,1,0:T(2,128)(2,1)} copy(bf16[1792,2,256]{0,2,1:T(8,128)(2,1)S(1)} %pad_maximum_fusion.1) | data formatting | bytes 3670016
  308.3 28.3 %all-gather.15.cloned.1.call-done = bf16[14,64,1024]{2,1,0:T(8,128)(2,1)} async-done(((bf16[14,16,1024]{2,1,0:T(8,128)(2,1)}), bf16[14,64,1024]{2,1,0:T(8,128)(2,1)}) %all-gather.15.cloned.1.call-update) | async-done | bytes 1835024 | tf_op jit(solution)/shard_map/all_gather | solution.py:205
  336.6 4.6 %pad_maximum_fusion = bf16[14,4,32,1024]{3,2,1,0:T(8,128)(2,1)} fusion(bf16[14,4,16,1024]{3,2,1,0:T(8,128)(2,1)} %bitcast.160, bf16[14,4,16,1024]{3,2,1,0:T(8,128)(2,1)} %bitcast.161), kind=kLoop, calls=%fused_computation.18 | loop fusion | flops 7340032 | bytes 7340032 | tf_op jit(solution)/shard_map/concatenate | solution.py:206
  (77 shorter events, 9.8 us)
Async XLA Ops:
  7.2 8.7 %copy-start.2 = (bf16[129,256]{1,0:T(8,128)(2,1)S(1)}, bf16[129,256]{1,0:T(8,128)(2,1)}, u32[]{:S(2)}) copy-start(bf16[129,256]{1,0:T(8,128)(2,1)} %constant.158.clone.1) | copy-start | bytes 198148
  7.2 57.3 %all-gather.9.cloned.1.call-start = ((), (), s32[]{:S(2)}) async-start(), calls=%async_computation.4 | async-start | bytes 1622016 | tf_op jit(solution)/shard_map/all_gather | solution.py:85
  8.6 102.5 %all-gather.11.cloned.1.call-start = ((), (), s32[]{:S(2)}) async-start(), calls=%async_computation.5 | async-start | bytes 4587520 | tf_op jit(solution)/shard_map/all_gather | solution.py:123
  12.1 5.2 %copy-start.3 = (bf16[1024,32]{0,1:T(8,128)(2,1)S(1)}, bf16[1024,32]{0,1:T(8,128)(2,1)}, u32[]{:S(2)}) copy-start(bf16[1024,32]{0,1:T(8,128)(2,1)} %param.27) | copy-start | bytes 196612
  12.1 5.2 %copy-start.4 = (bf16[32,1024]{1,0:T(8,128)(2,1)S(1)}, bf16[32,1024]{1,0:T(8,128)(2,1)}, u32[]{:S(2)}) copy-start(bf16[32,1024]{1,0:T(8,128)(2,1)} %param.26) | copy-start | bytes 196612
  12.1 5.2 %copy-start.8 = (bf16[256,32]{0,1:T(8,128)(2,1)S(1)}, bf16[256,32]{0,1:T(8,128)(2,1)}, u32[]{:S(2)}) copy-start(bf16[256,32]{0,1:T(8,128)(2,1)} %param.25) | copy-start | bytes 49156
  58.2 1.4 copy-start
  64.5 129.2 %all-gather.13.cloned.1.call-start = ((), (), s32[]{:S(2)}) async-start(), calls=%async_computation.6 | async-start | bytes 19464192 | tf_op jit(solution)/shard_map/all_gather | solution.py:126
  112.6 6.9 %copy-start.5 = (s32[1,1,14,128]{3,1,2,0:T(1,128)}, s32[1,1,14,128]{3,1,2,0:T(1,128)S(1)}, u32[]{:S(2)}) copy-start(s32[1,1,14,128]{3,1,2,0:T(1,128)S(1)} %copy.46) | copy-start | bytes 21508
  164.3 15.6 %all-to-all-start.1 = ((bf16[14,4,32,256]{3,2,0,1:T(8,128)(2,1)}), bf16[14,4,32,256]{3,2,0,1:T(8,128)(2,1)}, u32[]{:S(2)}, u32[]{:S(2)}) async-start(bf16[14,4,32,256]{3,2,0,1:T(8,128)(2,1)} %copy.36), calls=%async_computation.1 | async-start | bytes 1835008 | tf_op jit(solution)/shard_map/all_to_all | solution.py:148
  198.5 2.7 copy-start.9
  198.5 2.7 copy-start.10
  221.4 2.9 copy-start.6
  221.4 2.9 copy-start.7
  242.9 4.8 %copy-start.1 = (bf16[14,16,1024]{2,1,0:T(8,128)(2,1)S(1)}, bf16[14,16,1024]{2,1,0:T(8,128)(2,1)}, u32[]{:S(2)}) copy-start(bf16[14,16,1024]{2,1,0:T(8,128)(2,1)} %slice.255) | copy-start | bytes 1376260
  254.7 22.6 %all-to-all-start.3 = ((bf16[32,16,1024]{2,1,0:T(8,128)(2,1)}), bf16[32,16,1024]{2,1,0:T(8,128)(2,1)}, u32[]{:S(2)}, u32[]{:S(2)}) async-start(bf16[32,16,1024]{2,1,0:T(8,128)(2,1)} %broadcast_select_fusion), calls=%async_computation.3 | async-start | bytes 2097152 | tf_op jit(solution)/shard_map/all_to_all | solution.py:203
  260.2 48.1 %all-gather.17.cloned.1.call-start = ((), (), s32[]{:S(2)}) async-start(), calls=%async_computation.8 | async-start | bytes 2293760 | tf_op jit(solution)/shard_map/all_gather | solution.py:205
  279.9 56.7 %all-gather.15.cloned.1.call-start = ((), (), s32[]{:S(2)}) async-start(), calls=%async_computation.7 | async-start | bytes 2293760 | tf_op jit(solution)/shard_map/all_gather | solution.py:205
Sparse Core Ops, SparseCore 0:
  10.2 54.1 all-gather.8
  66.7 44.3 all-gather.10
  113.4 80.2 all-gather.12
  280.0 25.8 all-gather.16
  308.0 28.5 all-gather.14

commit v5 on v3

--- a/solution.py
+++ b/solution.py
@@ -2,6 +2,7 @@
 import jax.numpy as jnp
 from jax import lax
 from jax.experimental import pallas as pl
+from jax.experimental.pallas import tpu as pltpu
 from jax.sharding import PartitionSpec as P
 
 HEAD = 64
@@ -13,43 +14,99 @@
     return center * lax.rsqrt(spread + 1e-05) * gain + shift
 
 
-def _attn_kernel(q_ref, k_ref, v_ref, qid_ref, kid_ref, o_ref):
-    same = qid_ref[...] == kid_ref[...]
+KEY_CHUNK = 256
+
+
+def _attn_kernel(lo_ref, hi_ref, q_ref, k_ref, v_ref, qid_ref, kid_ref, o_ref, s_ref, m_ref, l_ref, acc_ref):
+    block = pl.program_id(0)
+    lo = lo_ref[block]
+    hi = hi_ref[block]
+    chunks = k_ref.shape[1] // KEY_CHUNK
+    qid = qid_ref[...]
     for head in range(q_ref.shape[0]):
-        scores = lax.dot_general(
-            q_ref[head], k_ref[head], (((1,), (1,)), ((), ())), preferred_element_type=jnp.float32
-        ) * (HEAD ** -0.5)
-        scores = jnp.where(same, scores, -1e30)
-        highest = jnp.max(scores, axis=1, keepdims=True)
-        raised = jnp.exp(scores - highest)
-        weights = (raised / jnp.sum(raised, axis=1, keepdims=True)).astype(jnp.bfloat16)
-        o_ref[:, head * HEAD : (head + 1) * HEAD] = jnp.dot(
-            weights, v_ref[head], preferred_element_type=jnp.float32
-        ).astype(o_ref.dtype)
+        q = q_ref[head]
+        m_ref[...] = jnp.full(m_ref.shape, -jnp.inf, jnp.float32)
+        l_ref[...] = jnp.zeros(l_ref.shape, jnp.float32)
+        acc_ref[...] = jnp.zeros(acc_ref.shape, jnp.float32)
+        for c in range(chunks):
+            cols = slice(c * KEY_CHUNK, (c + 1) * KEY_CHUNK)
+
+            @pl.when((c >= lo) & (c < hi))
+            def _():
+                scores = lax.dot_general(
+                    q, k_ref[head, cols, :], (((1,), (1,)), ((), ())),
+                    preferred_element_type=jnp.float32,
+                ) * (HEAD ** -0.5)
+                scores = jnp.where(qid == kid_ref[:, cols], scores, -1e30)
+                s_ref[:, cols] = scores
+                m_ref[...] = jnp.maximum(m_ref[...], jnp.max(scores, axis=1, keepdims=True))
+
+        for c in range(chunks):
+            cols = slice(c * KEY_CHUNK, (c + 1) * KEY_CHUNK)
+
+            @pl.when((c >= lo) & (c < hi))
+            def _():
+                raised = jnp.exp(s_ref[:, cols] - m_ref[...])
+                s_ref[:, cols] = raised
+                l_ref[...] = l_ref[...] + jnp.sum(raised, axis=1, keepdims=True)
+
+        for c in range(chunks):
+            cols = slice(c * KEY_CHUNK, (c + 1) * KEY_CHUNK)
+
+            @pl.when((c >= lo) & (c < hi))
+            def _():
+                weights = (s_ref[:, cols] / l_ref[...]).astype(jnp.bfloat16)
+                acc_ref[...] = acc_ref[...] + jnp.dot(
+                    weights, v_ref[head, cols, :], preferred_element_type=jnp.float32
+                )
+
+        o_ref[:, head * HEAD : (head + 1) * HEAD] = acc_ref[...].astype(o_ref.dtype)
+
+
+def key_ranges(ids, block_q):
+    rows = ids.shape[0]
+    index = jnp.arange(rows, dtype=jnp.int32)
+    new_run = jnp.concatenate([jnp.ones((1,), bool), ids[1:] != ids[:-1]])
+    run_start = lax.cummax(jnp.where(new_run, index, 0))
+    run_last = jnp.concatenate([ids[1:] != ids[:-1], jnp.ones((1,), bool)])
+    run_end = lax.cummin(jnp.where(run_last, index + 1, rows), reverse=True)
+    lo = run_start[::block_q] // KEY_CHUNK
+    hi = (run_end[block_q - 1 :: block_q] + KEY_CHUNK - 1) // KEY_CHUNK
+    return lo.astype(jnp.int32), hi.astype(jnp.int32)
 
 
 def attention(q, k, v, ids, block_q=256):
     heads, rows, dim = q.shape
+    lo, hi = key_ranges(ids, block_q)
     qid = ids.reshape(rows, 1)
     kid = ids.reshape(1, rows)
     return pl.pallas_call(
         _attn_kernel,
         out_shape=jax.ShapeDtypeStruct((rows, heads * dim), jnp.bfloat16),
-        grid=(rows // block_q,),
-        in_specs=[
-            pl.BlockSpec((heads, block_q, dim), lambda i: (0, i, 0)),
-            pl.BlockSpec((heads, rows, dim), lambda i: (0, 0, 0)),
-            pl.BlockSpec((heads, rows, dim), lambda i: (0, 0, 0)),
-            pl.BlockSpec((block_q, 1), lambda i: (i, 0)),
-            pl.BlockSpec((1, rows), lambda i: (0, 0)),
-        ],
-        out_specs=pl.BlockSpec((block_q, heads * dim), lambda i: (i, 0)),
+        grid_spec=pltpu.PrefetchScalarGridSpec(
+            num_scalar_prefetch=2,
+            grid=(rows // block_q,),
+            in_specs=[
+                pl.BlockSpec((heads, block_q, dim), lambda i, lo, hi: (0, i, 0)),
+                pl.BlockSpec((heads, rows, dim), lambda i, lo, hi: (0, 0, 0)),
+                pl.BlockSpec((heads, rows, dim), lambda i, lo, hi: (0, 0, 0)),
+                pl.BlockSpec((block_q, 1), lambda i, lo, hi: (i, 0)),
+                pl.BlockSpec((1, rows), lambda i, lo, hi: (0, 0)),
+            ],
+            out_specs=pl.BlockSpec((block_q, heads * dim), lambda i, lo, hi: (i, 0)),
+            scratch_shapes=[
+                pltpu.VMEM((block_q, rows), jnp.float32),
+                pltpu.VMEM((block_q, 1), jnp.float32),
+                pltpu.VMEM((block_q, 1), jnp.float32),
+                pltpu.VMEM((block_q, dim), jnp.float32),
+            ],
+        ),
         cost_estimate=pl.CostEstimate(
-            flops=4 * heads * rows * rows * dim,
-            transcendentals=heads * rows * rows,
+            flops=2 * heads * rows * rows * dim,
+            transcendentals=heads * rows * rows // 2,
             bytes_accessed=4 * heads * rows * dim * 2,
         ),
-    )(q, k, v, qid, kid)
+    )(lo, hi, q, k, v, qid, kid)
 
 
 def body(

time: 324 us -> 402 us (1.24); the launches traced: 323 us -> 396 us
  Pallas kernels: 32.9 us -> 81.7 us
  starting transfers between devices: 9.69 us -> 47.8 us
  waiting for transfers between devices: 83.3 us -> 65 us
    pallas_call x1, Pallas kernels: 32.9 us -> 81.7 us  [attention(): pl.pallas_call(_attn_kernel, out_shape=jax.ShapeDtypeStruct((rows, heads...]
    all_to_all x1, starting transfers between devices: 5.4 us -> 43.8 us  [body(): lax.all_to_all(outgoing, 'dp', split_axis=0, concat_axis=0, tiled=True)]
    all_gather x1, waiting for transfers between devices: 14.9 us -> 0.01 us  [body(): ffn_gathered = lax.all_gather(ffn_local, 'dp', axis=0, tiled=True)]
  transfers between devices with their start and end apart: 7 -> 7, of which waited for: 5 -> 4; matrix products, arithmetic and copies ran while one was open for 20% -> 18% of each run, Pallas kernels for 10% -> 21%
where the time goes in v5:
time: 402 us; the launch traced here: 396 us
  Pallas kernels  81.7 us (20%)
  blocking collectives  76.4 us (19%)
  waiting for transfers between devices  65 us (16%)
  matrix products  62.1 us (15%)
  starting transfers between devices  47.8 us (12%)
  local copies, waits for them, and re-layouts  25.2 us (6%)
  other arithmetic  22.7 us (6%)
  between operations  14.8 us (4%)
    pallas_call x1, Pallas kernels, attention(): pl.pallas_call(_attn_kernel, out_shape=jax.ShapeDtypeStruct((rows, heads...  81.7 us
    all_to_all x1, starting transfers between devices, body(): lax.all_to_all(outgoing, 'dp', split_axis=0, concat_axis=0, tiled=True)  43.8 us
    all_to_all x1, blocking collectives, body(): lax.all_to_all(send_pages, 'dp', split_axis=0, concat_axis=0, tiled=True)  40.9 us
    all_gather x1, waiting for transfers between devices, body(): lax.all_gather(dealt_part, 'mp', axis=2, tiled=True)  33.4 us
    all_to_all x1, blocking collectives, body(): lax.all_to_all(outgoing, 'dp', split_axis=0, concat_axis=0, tiled=True)  24.2 us
    dot_general x2, matrix products, feed_forward(): jnp.einsum('pid,du->piu', first_rows, full_up, preferred_element_type=jnp...  24.1 us
    dot_general x8, matrix products, feed_forward(): jnp.einsum('piu,ou->pio', hidden[:, :, group * unit_part:(group + 1) * un...  21.5 us
    all_gather x2, waiting for transfers between devices, body(): pieces = [lax.all_gather(part, 'mp', axis=1) for part in pieces]  21.2 us
  transfers between devices with their start and end apart: 7, of which 4 were waited for; matrix products, arithmetic and copies ran while one was open for 18% of the time, Pallas kernels for 21%

profile of v5, /device:TPU:1, one launch (start us, length us, event | category | flops | bytes accessed | tf_op | source)
XLA Modules:
  0.0 395.8 jit_solution(7352332467265844202)
XLA Ops:
  7.2 1.4 pad_maximum_fusion.5
  10.9 1.4 and_reduce_fusion
  12.3 1.4 broadcast_select_fusion.2
  14.4 1.2 constant_dynamic-slice_fusion
  15.9 1.3 scatter_fusion
  17.3 40.9 %all_to_all.20 = bf16[32,129,256]{2,1,0:T(8,128)(2,1)S(1)} all-to-all(bf16[32,129,256]{2,1,0:T(8,128)(2,1)S(1)} %scatter_fusion), channel_id=1, replica_groups=mesh['dp'=32,'mp'=4] {'dp'}, dimensions={0} | all-to-all | bytes 4227072 | tf_op jit(solution)/shard_map/all_to_all | solution.py:167
  58.5 1.1 copy-done
  59.6 1.2 clamp_reduce_fusion
  60.9 1.5 gather_fusion
  62.5 2.9 all-gather.9.cloned.1.call-done
  65.4 11.3 %all-gather = bf16[32,9216]{1,0:T(8,128)(2,1)S(1)} all-gather(bf16[32,2304]{1,0:T(8,128)(2,1)S(1)} %pad_maximum_fusion.4), channel_id=2, replica_groups=mesh['dp'=32,'mp'=4] {'mp'}, dimensions={1}, use_global_device_ids=true | all-gather | bytes 737280 | tf_op jit(solution)/shard_map/all_gather | solution.py:175
  78.5 33.4 %all-gather.11.cloned.1.call-done = bf16[14,128,1024]{2,1,0:T(8,128)(2,1)} async-done(((bf16[14,128,256]{2,1,0:T(8,128)(2,1)}), bf16[14,128,1024]{2,1,0:T(8,128)(2,1)}) %all-gather.11.cloned.1.call-update) | async-done | bytes 3670032 | tf_op jit(solution)/shard_map/all_gather | solution.py:183
  114.2 2.3 reduce-window.24
  116.9 1.3 copy.49
  118.7 3.3 convolution_convert_fusion.2
  122.0 1.8 copy.38
  123.9 3.4 convolution_convert_fusion.1
  127.2 1.7 copy.39
  128.9 3.3 convolution_convert_fusion
  132.2 1.7 copy.40
  133.9 81.7 %shard_map.140 = bf16[1792,256]{1,0:T(8,128)(2,1)} custom-call(s32[7]{0:T(128)} %get-tuple-element.73.lo_ref, s32[7]{0:T(128)} %get-tuple-element.72.hi_ref, bf16[4,1792,64]{2,1,0:T(8,128)(2,1)} %bitcast.182, bf16[4,1792,64]{2,1,0:T(8,128)(2,1)} %bitcast.183, bf16[4,1792,64]{2,1,0:T(8,128)(2,1)} %bitcast.184, s32[1792,1]{1,0:T(8,128)} %bitcast.190, ...), custom_call_target="tpu_custom_call" | custom-call | flops 1644167168 | bytes 3670016 | tf_op jit(solution)/shard_map/pallas_call | solution.py:83
  215.7 2.2 copy.42
  217.8 3.8 all-to-all-start.1
  221.7 1.5 compare_reduce_fusion
  223.2 7.5 %all-to-all-done.1 = bf16[14,4,32,256]{3,2,0,1:T(8,128)(2,1)S(1)} async-done(((bf16[14,4,32,256]{3,2,0,1:T(8,128)(2,1)}), bf16[14,4,32,256]{3,2,0,1:T(8,128)(2,1)S(1)}, u32[]{:S(2)}, u32[]{:S(2)}) %all-to-all-start.1) | async-done | bytes 917536 | tf_op jit(solution)/shard_map/all_to_all | solution.py:204
  230.7 1.5 convolution_convert_fusion.4
  232.2 1.5 convolution_convert_fusion.5
  233.7 1.5 convolution_convert_fusion.6
  235.2 2.2 fusion.76
  238.1 11.9 %fusion.4 = bf16[14,16,4096]{2,1,0:T(8,128)(2,1)S(1)} fusion(bf16[1024,9216]{1,0:T(8,128)(2,1)} %all-gather.13.cloned.1.call-done, bf16[14,32,1024]{2,1,0:T(8,128)(2,1)S(1)} %add_convert_fusion), kind=kOutput, calls=%fused_computation.14 | convolution fusion | flops 1938685952 | bytes 10682368 | tf_op jit(solution)/shard_map/pid,du->piu/dot_general | solution.py:228
  250.0 2.4 fusion.53
  252.4 2.4 fusion.51
  254.8 2.4 fusion.49
  257.2 2.6 fusion.77
  261.0 1.1 broadcast_select_fusion.1
  262.1 43.8 %all-to-all-start.2 = ((bf16[32,16,1024]{2,1,0:T(8,128)(2,1)}), bf16[32,16,1024]{2,1,0:T(8,128)(2,1)S(1)}, u32[]{:S(2)}, u32[]{:S(2)}) async-start(bf16[32,16,1024]{2,1,0:T(8,128)(2,1)} %broadcast_select_fusion.1), calls=%async_computation.2 | async-start | bytes 2097152 | tf_op jit(solution)/shard_map/all_to_all | solution.py:259
  305.9 12.2 %fusion.7 = bf16[14,16,4096]{2,1,0:T(8,128)(2,1)S(1)} fusion(bf16[14,16,1024]{2,1,0:T(8,128)(2,1)S(1)} %slice.289, bf16[1024,9216]{1,0:T(8,128)(2,1)} %all-gather.13.cloned.1.call-done), kind=kOutput, calls=%fused_computation.17 | convolution fusion | flops 1938685952 | bytes 10682368 | tf_op jit(solution)/shard_map/pid,du->piu/dot_general | solution.py:228
  318.1 3.0 fusion.52
  321.2 3.3 fusion.50
  324.5 1.4 gather_fusion.3
  326.0 2.6 fusion.48
  328.6 2.8 fusion.78
  332.6 24.2 %all_to_all.21 = bf16[32,16,1024]{2,1,0:T(8,128)(2,1)S(1)} all-to-all(bf16[32,16,1024]{2,1,0:T(8,128)(2,1)S(1)} %broadcast_select_fusion), channel_id=1, replica_groups=mesh['dp'=32,'mp'=4] {'dp'}, dimensions={0} | all-to-all | bytes 2097152 | tf_op jit(solution)/shard_map/all_to_all | solution.py:259
  356.8 1.3 gather_fusion.5
  358.2 1.3 pad_maximum_fusion.1
  359.6 3.6 copy.43
  363.1 21.2 %all-gather.17.cloned.1.call-done = bf16[14,64,1024]{2,1,0:T(8,128)(2,1)} async-done(((bf16[14,16,1024]{2,1,0:T(8,128)(2,1)}), bf16[14,64,1024]{2,1,0:T(8,128)(2,1)}) %all-gather.17.cloned.1.call-update) | async-done | bytes 1835024 | tf_op jit(solution)/shard_map/all_gather | solution.py:261
  384.3 4.6 %pad_maximum_fusion = bf16[14,4,32,1024]{3,2,1,0:T(8,128)(2,1)} fusion(bf16[14,4,16,1024]{3,2,1,0:T(8,128)(2,1)} %bitcast.181, bf16[14,4,16,1024]{3,2,1,0:T(8,128)(2,1)} %bitcast.180), kind=kLoop, calls=%fused_computation.18 | loop fusion | flops 7340032 | bytes 7340032 | tf_op jit(solution)/shard_map/concatenate | solution.py:262
  (97 shorter events, 11.9 us)
Async XLA Ops:
  7.2 8.6 %copy-start.4 = (bf16[129,256]{1,0:T(8,128)(2,1)S(1)}, bf16[129,256]{1,0:T(8,128)(2,1)}, u32[]{:S(2)}) copy-start(bf16[129,256]{1,0:T(8,128)(2,1)} %constant.188.clone.1) | copy-start | bytes 198148
  7.2 58.2 %all-gather.9.cloned.1.call-start = ((), (), s32[]{:S(2)}) async-start(), calls=%async_computation.4 | async-start | bytes 1622016 | tf_op jit(solution)/shard_map/all_gather | solution.py:142
  8.6 103.3 %all-gather.11.cloned.1.call-start = ((), (), s32[]{:S(2)}) async-start(), calls=%async_computation.5 | async-start | bytes 4587520 | tf_op jit(solution)/shard_map/all_gather | solution.py:183
  15.7 1.6 copy-start.5
  15.7 1.6 copy-start.6
  15.7 1.6 copy-start.10
  58.2 1.4 copy-start
  65.4 165.3 %all-gather.13.cloned.1.call-start = ((), (), s32[]{:S(2)}) async-start(), calls=%async_computation.6 | async-start | bytes 19464192 | tf_op jit(solution)/shard_map/all_gather | solution.py:186
  113.4 8.7 %copy-start.7 = (s32[1,1,14,128]{3,1,2,0:T(1,128)}, s32[1,1,14,128]{3,1,2,0:T(1,128)S(1)}, u32[]{:S(2)}) copy-start(s32[1,1,14,128]{3,1,2,0:T(1,128)S(1)} %copy.52) | copy-start | bytes 21508
  132.2 83.5 %copy-start.1 = (bf16[1792,256]{0,1:T(8,128)(2,1)}, bf16[1792,256]{0,1:T(8,128)(2,1)S(1)}, u32[]{:S(2)}) copy-start(bf16[1792,256]{0,1:T(8,128)(2,1)S(1)} %convolution_convert_fusion) | copy-start | bytes 2752516
  217.8 12.8 %all-to-all-start.1 = ((bf16[14,4,32,256]{3,2,0,1:T(8,128)(2,1)}), bf16[14,4,32,256]{3,2,0,1:T(8,128)(2,1)S(1)}, u32[]{:S(2)}, u32[]{:S(2)}) async-start(bf16[14,4,32,256]{3,2,0,1:T(8,128)(2,1)} %copy.42), calls=%async_computation.1 | async-start | bytes 1835008 | tf_op jit(solution)/shard_map/all_to_all | solution.py:204
  235.1 2.5 copy-start.11
  235.2 2.5 copy-start.12
  257.2 2.9 copy-start.8
  257.2 2.9 copy-start.9
  262.1 62.4 %all-to-all-start.2 = ((bf16[32,16,1024]{2,1,0:T(8,128)(2,1)}), bf16[32,16,1024]{2,1,0:T(8,128)(2,1)S(1)}, u32[]{:S(2)}, u32[]{:S(2)}) async-start(bf16[32,16,1024]{2,1,0:T(8,128)(2,1)} %broadcast_select_fusion.1), calls=%async_computation.2 | async-start | bytes 2097152 | tf_op jit(solution)/shard_map/all_to_all | solution.py:259
  305.9 57.2 %all-gather.15.cloned.1.call-start = ((), (), s32[]{:S(2)}) async-start(), calls=%async_computation.7 | async-start | bytes 2293760 | tf_op jit(solution)/shard_map/all_gather | solution.py:261
  318.1 3.1 copy-start.3
  325.9 2.7 copy-start.2
  325.9 58.4 %all-gather.17.cloned.1.call-start = ((), (), s32[]{:S(2)}) async-start(), calls=%async_computation.8 | async-start | bytes 2293760 | tf_op jit(solution)/shard_map/all_gather | solution.py:261
Sparse Core Ops, SparseCore 0:
  10.2 55.0 all-gather.8
  67.6 44.2 all-gather.10
  114.1 80.3 all-gather.12
  326.0 27.5 all-gather.14
  358.3 25.9 all-gather.16
